TPU v7x, 128 devices: a whole 4x4x4 slice. The times are simulated.
128 devices in a mesh: gx: 16 (over x_hi, z, core), gy: 8 (over x_lo, y).
Axes of the slice: x: 4 (x_hi: 2, x_lo: 2; x = x_hi * 2 + x_lo), y: 4, z: 4, core: 2. Of those that a mesh axis runs over, the one named last changes fastest.
Arguments:
- patches: bfloat16 [8, 64, 256, 1024], P(None, None, 'gx', 'gy'), may hold values from -6 to 6
- patch_wx: bfloat16 [8, 8, 256], P(None, 'gy', 'gx'), may hold values from 1 to 3
- patch_wy: bfloat16 [8, 16, 1024], P(None, 'gx', 'gy'), may hold values from 1 to 3
- offset_x: int32 [8, 16, 8], P(None, 'gx', 'gy'), may hold values from 0 to 15
- offset_y: int32 [8, 16, 8], P(None, 'gx', 'gy'), may hold values from 0 to 127
- block_counts: int32 [16, 8], P('gx', 'gy'), may hold values from 2 to 8, as said below
- template: bfloat16 [64, 256, 1024], P(None, 'gx', 'gy'), may hold values from -6 to 6
- stiff_mu: float32 [64, 256, 1024], P(None, 'gx', 'gy'), may hold values from 0.5 to 2
- stiff_lam: float32 [64, 256, 1024], P(None, 'gx', 'gy'), may hold values from 0.5 to 4
- start_field: float32 [3, 64, 256, 1024], P(None, None, 'gx', 'gy'), may hold values from -4 to 4
Outputs:
- joined: bfloat16 [64, 256, 1024], P(None, 'gx', 'gy')
- field: float32 [3, 64, 256, 1024], P(None, None, 'gx', 'gy')
Inputs may be any that keep to these rules, and one draw needn't show every extreme that they name: `block_counts`: a block's patch slots at or beyond its count are unused; some block holds exactly 8 live patches.
All inputs are finite; a program needn't handle non-finite values.
Results may differ from a plain program's by a relative error of at most 0.0045.
Values may be sent and summed in bfloat16 or wider, within the bound.
No kernel may reach another device: no remote copies, remote signals or barrier semaphores. Data moves between devices by JAX's collectives and lax.ppermute only.
A program may use at most 128 MiB of HBM per device.

v0:
```python
import jax
import jax.numpy as jnp
from jax import lax
from jax.experimental import pallas as pl
from jax.experimental.pallas import tpu as pltpu
from jax.sharding import PartitionSpec as P

PASSES = 4


RELAX_FACTOR = 0.9
STEPS_UNIT = ((1, 0, 0), (0, 1, 0), (0, 0, 1))
EXACT = lax.Precision.HIGHEST
HALF = 8


def shifted_in(block, axis, distance):
    count = lax.axis_size(axis)
    route = [(i, i + distance) for i in range(count) if 0 <= i + distance < count]
    return lax.ppermute(block, axis, route)


def diagonal_in(block):
    nx = lax.axis_size("gx")
    ny = lax.axis_size("gy")
    route = [(i * ny + j, (i + 1) * ny + j + 1) for i in range(nx - 1) for j in range(ny - 1)]
    return lax.ppermute(block, ("gx", "gy"), route)


def edge_lanes(wide_y):
    lanes = jnp.array([0, 1, wide_y - 2, wide_y - 1], jnp.int32)
    return (lax.broadcasted_iota(jnp.int32, (4, wide_y), 1) == lanes[:, None]).astype(jnp.float32)


def halo(v):
    chans, depth, wide_x, wide_y = v.shape
    pick = edge_lanes(wide_y)
    rows = v.reshape(chans * depth * wide_x, wide_y)
    strips = jnp.einsum("ky,ry->kr", pick, rows, precision=EXACT)
    y_high = shifted_in(strips[:2], "gy", -1)
    y_low = shifted_in(strips[2:], "gy", 1)
    arrived = jnp.concatenate([y_high, y_low], axis=0)
    wrapped = jnp.einsum("kr,ky->ry", arrived, pick, precision=EXACT).reshape(v.shape)
    upward = jnp.concatenate([v[:, :, wide_x - 2 :], wrapped[:, :, wide_x - 2 :]], axis=2)
    downward = jnp.concatenate([v[:, :, :2], wrapped[:, :, :2]], axis=2)
    x_low = shifted_in(upward, "gx", 1)
    x_high = shifted_in(downward, "gx", -1)
    z_pad = ((0, 0), (2, 2), (0, 0), (0, 0))
    xe = jnp.pad(jnp.concatenate([x_low[:, :, :2], v, x_high[:, :, :2]], axis=2), z_pad)
    fe = jnp.pad(jnp.concatenate([x_low[:, :, 2:], wrapped, x_high[:, :, 2:]], axis=2), z_pad)
    return xe, fe


def full_pad(xe, fe):
    wide_y = xe.shape[-1]
    return jnp.concatenate([fe[..., wide_y - 2 :], xe, fe[..., :2]], axis=-1)


def window(array_in, move_z, move_x, move_y):
    size_z = array_in.shape[-3] - 4
    size_x = array_in.shape[-2] - 4
    size_y = array_in.shape[-1] - 4
    return array_in[
        ...,
        2 + move_z : 2 + move_z + size_z,
        2 + move_x : 2 + move_x + size_x,
        2 + move_y : 2 + move_y + size_y,
    ]


def placement(starts, slots, wide):
    source = lax.broadcasted_iota(jnp.int32, (slots, wide, 2 * wide), 1)
    target = lax.broadcasted_iota(jnp.int32, (slots, wide, 2 * wide), 2)
    return (target == source + starts.astype(jnp.int32)[:, None, None]).astype(jnp.float32)


def blend_home(patches, patch_wx, patch_wy, offset_x, offset_y, live_count):
    slots, depth_z, wide_x, wide_y = patches.shape
    slot_ids = lax.broadcasted_iota(jnp.int32, (slots,), 0)
    live = (slot_ids < live_count[0, 0]).astype(jnp.float32)
    place_x = placement(offset_x[:, 0, 0], slots, wide_x)
    place_y = placement(offset_y[:, 0, 0], slots, wide_y)
    along_x = patch_wx[:, 0, :].astype(jnp.float32) * live[:, None]
    along_y = patch_wy[:, 0, :].astype(jnp.float32)
    scaled = patches.astype(jnp.float32) * along_x[:, None, :, None] * along_y[:, None, None, :]
    wide_rows = jnp.einsum("szxy,syY->szxY", scaled, place_y, precision=EXACT)
    weighted = jnp.einsum("szxY,sxX->zXY", wide_rows, place_x, precision=EXACT)
    row_weight = jnp.einsum("sx,sxX->sX", along_x, place_x, precision=EXACT)
    col_weight = jnp.einsum("sy,syY->sY", along_y, place_y, precision=EXACT)
    weight_sum = jnp.einsum("sX,sY->XY", row_weight, col_weight, precision=EXACT)
    return (weighted, weight_sum)


def relax_kernel(xe_ref, fe_ref, mc_ref, bc_ref, rate_ref, force_ref, out_ref):
    chunk = out_ref.shape[1]
    wide_x = out_ref.shape[2]
    wide_y = out_ref.shape[3]
    first = pl.program_id(0) * chunk
    lane = lax.broadcasted_iota(jnp.int32, (HALF, wide_y), 1)
    inside = {dy: (lane + dy >= 0) & (lane + dy < wide_y) for dy in (-2, -1, 1, 2)}

    def body(z, carry):
        plane = first + z + 2
        for half in range(wide_x // HALF):
            rows = pl.ds(half * HALF, HALF)
            rate = rate_ref[z, rows, :]
            for comp in range(3):
                cache = {}

                def val(c, dz, dx, dy):
                    key = (c, dz, dx, dy)
                    if key not in cache:
                        span = pl.ds(2 + dx + half * HALF, HALF)
                        got = xe_ref[c, plane + dz, span, :]
                        if dy != 0:
                            ring = fe_ref[c, plane + dz, span, :]
                            turn = (-dy) % wide_y
                            got = jnp.where(
                                inside[dy], pltpu.roll(got, turn, 1), pltpu.roll(ring, turn, 1)
                            )
                        cache[key] = got
                    return cache[key]

                centre = val(comp, 0, 0, 0)
                laplace = 0.0
                for dim in range(3):
                    ahead = STEPS_UNIT[dim]
                    behind = tuple(-t for t in ahead)
                    laplace = laplace + mc_ref[2 * dim, z, rows, :] * (val(comp, *ahead) - centre)
                    laplace = laplace - mc_ref[2 * dim + 1, z, rows, :] * (
                        centre - val(comp, *behind)
                    )
                step = STEPS_UNIT[comp]

                def divergence(sign):
                    result = 0.0
                    for dim in range(3):
                        unit = STEPS_UNIT[dim]
                        fwd = tuple(sign * step[k] + unit[k] for k in range(3))
                        bwd = tuple(sign * step[k] - unit[k] for k in range(3))
                        result = result + 0.5 * (val(dim, *fwd) - val(dim, *bwd))
                    return result

                grad_div = 0.5 * (
                    bc_ref[2 * comp, z, rows, :] * divergence(1)
                    - bc_ref[2 * comp + 1, z, rows, :] * divergence(-1)
                )
                out_ref[comp, z, rows, :] = centre + rate * (
                    laplace + grad_div + force_ref[comp, z, rows, :]
                )
        return carry

    lax.fori_loop(0, chunk, body, 0)


def relax_call(xe, fe, mc, bc, rate, forcing, chunk=8):
    chans, depth, wide_x, wide_y = forcing.shape
    out_shape = jax.ShapeDtypeStruct(forcing.shape, jnp.float32)
    moved = sum(a.size * a.dtype.itemsize for a in (xe, fe, mc, bc, rate, forcing)) + forcing.size * 4
    whole = pl.BlockSpec(xe.shape, lambda g: (0, 0, 0, 0))
    six = pl.BlockSpec((mc.shape[0], chunk, wide_x, wide_y), lambda g: (0, g, 0, 0))
    three = pl.BlockSpec((chans, chunk, wide_x, wide_y), lambda g: (0, g, 0, 0))
    one = pl.BlockSpec((chunk, wide_x, wide_y), lambda g: (g, 0, 0))
    return pl.pallas_call(
        relax_kernel,
        out_shape=out_shape,
        grid=(depth // chunk,),
        in_specs=[whole, whole, six, six, one, three],
        out_specs=three,
        compiler_params=pltpu.CompilerParams(vmem_limit_bytes=48 * 1024 * 1024),
        cost_estimate=pl.CostEstimate(
            flops=forcing.size * 70, transcendentals=0, bytes_accessed=moved
        ),
    )(xe, fe, mc, bc, rate, forcing)


def per_device(
    patches,
    patch_wx,
    patch_wy,
    offset_x,
    offset_y,
    block_counts,
    template,
    stiff_mu,
    stiff_lam,
    start_field,
):
    wide_x = patches.shape[2]
    wide_y = patches.shape[3]
    canvas, canvas_weight = blend_home(patches, patch_wx, patch_wy, offset_x, offset_y, block_counts)

    def quarter(upper_x, upper_y):
        cut_x = slice(upper_x * wide_x, (upper_x + 1) * wide_x)
        cut_y = slice(upper_y * wide_y, (upper_y + 1) * wide_y)
        return jnp.concatenate([canvas[:, cut_x, cut_y], canvas_weight[None, cut_x, cut_y]], axis=0)

    from_y = shifted_in(quarter(0, 1), "gy", 1)
    from_x = shifted_in(quarter(1, 0), "gx", 1)
    from_xy = diagonal_in(quarter(1, 1))
    total = quarter(0, 0) + from_y + from_x + from_xy
    weighted = total[:-1]
    weight_sum = total[-1]
    joined = (weighted / jnp.maximum(weight_sum, 1.0)[None]).astype(jnp.bfloat16)

    bulk = stiff_lam + stiff_mu
    rate = RELAX_FACTOR / (6.0 * stiff_mu + 3.0 * bulk)
    moduli = full_pad(*halo(jnp.stack([stiff_mu, bulk])))
    shear = moduli[0]
    bulk_pad = moduli[1]
    shear_here = window(shear, 0, 0, 0)
    mean_shear = []
    bulk_beside = []
    for dim in range(3):
        ahead = STEPS_UNIT[dim]
        behind = tuple(-t for t in ahead)
        mean_shear.append(0.5 * (shear_here + window(shear, *ahead)))
        mean_shear.append(0.5 * (shear_here + window(shear, *behind)))
        bulk_beside.append(window(bulk_pad, *ahead))
        bulk_beside.append(window(bulk_pad, *behind))
    mean_shear = jnp.stack(mean_shear)
    bulk_beside = jnp.stack(bulk_beside)

    image = full_pad(*halo(joined[None].astype(jnp.float32)))[0]
    centre = window(image, 0, 0, 0)
    mismatch = template.astype(jnp.float32) - centre
    slopes = []
    for dim in range(3):
        ahead = STEPS_UNIT[dim]
        behind = tuple(-t for t in ahead)
        slopes.append(0.5 * (window(image, *ahead) - window(image, *behind)) * mismatch)
    forcing = jnp.stack(slopes)

    def one_pass(pass_idx, field):
        xe, fe = halo(field)
        return relax_call(xe, fe, mean_shear, bulk_beside, rate, forcing)

    field = lax.fori_loop(0, PASSES, one_pass, start_field)
    return (joined, field)


def solution(mesh):
    placed = (
        P(None, None, "gx", "gy"),
        P(None, "gy", "gx"),
        P(None, "gx", "gy"),
        P(None, "gx", "gy"),
        P(None, "gx", "gy"),
        P("gx", "gy"),
        P(None, "gx", "gy"),
        P(None, "gx", "gy"),
        P(None, "gx", "gy"),
        P(None, None, "gx", "gy"),
    )
    return jax.shard_map(
        per_device,
        mesh=mesh,
        in_specs=placed,
        out_specs=(P(None, "gx", "gy"), P(None, None, "gx", "gy")),
        check_vma=False,
    )
```

profile of v0, /device:TPU:6, one launch (start us, length us, event | category | flops | bytes accessed | tf_op | source)
XLA Modules:
  0.0 271.0 jit_solution(5686177244423043563)
XLA Ops:
  3.5 5.2 %collective-permute-start.7 = (f32[2,2048]{1,0:T(2,128)S(1)}, f32[2,2048]{1,0:T(2,128)S(1)}, u32[]{:S(2)}, u32[]{:S(2)}) collective-permute-start(f32[2,2048]{1,0:T(2,128)S(1)} %get-tuple-element.166), channel_id=1, source_target_pairs={{1,0},{2,1},{3,2},{4,3},{5,4},{6,5},{7,6},{9,8},{10,9},{11,10},{12... | collective-permute-start | bytes 49160 | tf_op jit(solution)/shard_map/ppermute | solution.py:20
  8.7 1.9 collective-permute-start.8
  11.4 3.8 %fusion.9 = f32[8,64,16,256]{3,2,0,1:T(8,128)S(1)} fusion(s32[8]{0:T(128)S(1)} %bitcast.138, bf16[8,64,16,128]{3,2,1,0:T(8,128)(2,1)S(1)} %copy-done.7, f32[8,128]{1,0:T(8,128)S(1)} %bitcast_convert_fusion.1, f32[8,16]{1,0:T(8,128)S(1)} %convert_multiply_fusion), kind=kOutput, calls=%fused_computation.18 | convolution fusion | flops 3224895488 | bytes 10490400 | tf_op jit(solution)/shard_map/szxy,syY->szxY/dot_general | solution.py:86
  15.1 3.3 %convolution_bitcast_fusion = f32[64,32,256]{2,1,0:T(8,128)S(1)} fusion(f32[8,64,16,256]{3,2,0,1:T(8,128)S(1)} %fusion.9, s32[8]{0:T(128)S(1)} %bitcast.140), kind=kOutput, calls=%fused_computation.33 | convolution fusion | flops 805314560 | bytes 10485792 | tf_op jit(solution)/shard_map/szxY,sxX->zXY/dot_general | solution.py:87
  19.5 2.2 collective-permute-start.4
  23.8 1.9 collective-permute-start.9
  26.5 3.9 %collective-permute-start.5 = (f32[65,16,128]{2,1,0:T(8,128)}, f32[65,16,128]{2,1,0:T(8,128)}, u32[]{:S(2)}, u32[]{:S(2)}) collective-permute-start(f32[65,16,128]{2,1,0:T(8,128)} %pad_maximum_fusion.6), channel_id=1, source_target_pairs={{0,8},{8,16},{16,24},{24,32},{32,40},{40,48},{48,56},{56,64},{64,7... | collective-permute-start | bytes 1597448 | tf_op jit(solution)/shard_map/ppermute | solution.py:20
  31.3 5.2 %collective-permute-start.10 = (f32[2,64,4,128]{3,2,1,0:T(4,128)}, f32[2,64,4,128]{3,2,1,0:T(4,128)}, u32[]{:S(2)}, u32[]{:S(2)}) collective-permute-start(f32[2,64,4,128]{3,2,1,0:T(4,128)} %pad_maximum_fusion.9), channel_id=1, source_target_pairs={{8,0},{16,8},{24,16},{32,24},{40,32},{48,40},{56,48},{64,56},{72,6... | collective-permute-start | bytes 786440 | tf_op jit(solution)/shard_map/ppermute | solution.py:20
  37.4 2.1 collective-permute-start.6
  51.9 4.2 %collective-permute-done.6 = f32[65,16,128]{2,1,0:T(8,128)S(1)} collective-permute-done((f32[65,16,128]{2,1,0:T(8,128)}, f32[65,16,128]{2,1,0:T(8,128)S(1)}, u32[]{:S(2)}, u32[]{:S(2)}) %collective-permute-start.6) | collective-permute-done | bytes 532512 | tf_op jit(solution)/shard_map/ppermute | solution.py:27
  57.8 3.9 %collective-permute-start.11 = (f32[2,1024]{1,0:T(2,128)S(1)}, f32[2,1024]{1,0:T(2,128)S(1)}, u32[]{:S(2)}, u32[]{:S(2)}) collective-permute-start(f32[2,1024]{1,0:T(2,128)S(1)} %get-tuple-element.172), channel_id=1, source_target_pairs={{1,0},{2,1},{3,2},{4,3},{5,4},{6,5},{7,6},{9,8},{10,9},{11,10},{12... | collective-permute-start | bytes 24584 | tf_op jit(solution)/shard_map/ppermute | solution.py:20
  61.7 2.0 collective-permute-start.12
  64.0 5.3 %collective-permute-done.12 = f32[2,1024]{1,0:T(2,128)S(1)} collective-permute-done((f32[2,1024]{1,0:T(2,128)S(1)}, f32[2,1024]{1,0:T(2,128)S(1)}, u32[]{:S(2)}, u32[]{:S(2)}) %collective-permute-start.12) | collective-permute-done | bytes 8224 | tf_op jit(solution)/shard_map/ppermute | solution.py:20
  70.1 1.9 collective-permute-start.13
  72.5 7.5 %collective-permute-start.14 = (f32[1,64,4,128]{3,2,1,0:T(4,128)S(1)}, f32[1,64,4,128]{3,2,1,0:T(4,128)S(1)}, u32[]{:S(2)}, u32[]{:S(2)}) collective-permute-start(f32[1,64,4,128]{3,2,1,0:T(4,128)S(1)} %pad_maximum_fusion.11), channel_id=1, source_target_pairs={{8,0},{16,8},{24,16},{32,24},{40,32},{48,40},{56,48},{64,56},{72,6... | collective-permute-start | bytes 393224 | tf_op jit(solution)/shard_map/ppermute | solution.py:20
  80.1 2.2 collective-permute-done.14
  86.8 183.1 %while.13 = (s32[]{:T(128)}, f32[3,64,16,128]{3,2,1,0:T(8,128)S(1)}, f32[6,64,16,128]{3,2,1,0:T(8,128)}, f32[6,64,16,128]{3,2,1,0:T(8,128)}, f32[64,16,128]{2,1,...) while((s32[]{:T(128)}, f32[3,64,16,128]{3,2,1,0:T(8,128)S(1)}, ...), condition=%wide.region_1.2_spmd.clone, body=%wide.region_0.1_spmd.sunk.clone.sunk | while | flops 73839616 | bytes 54624616 | solution.py:238
  87.7 1.9 collective-permute-start
  89.6 6.0 %collective-permute-start.1 = (f32[2,3072]{1,0:T(2,128)S(1)}, f32[2,3072]{1,0:T(2,128)S(1)}, u32[]{:S(2)}, u32[]{:S(2)}) collective-permute-start(f32[2,3072]{1,0:T(2,128)S(1)} %get-tuple-element.226), channel_id=1, source_target_pairs={{1,0},{2,1},{3,2},{4,3},{5,4},{6,5},{7,6},{9,8},{10,9},{11,10},{12... | collective-permute-start | bytes 73736 | tf_op jit(solution)/shard_map/while/body/eval_jaxpr/ppermute | solution.py:20
  95.6 1.5 collective-permute-done.1
  99.9 1.9 collective-permute-start.3
  102.7 7.2 %collective-permute-start.2 = (f32[3,64,4,128]{3,2,1,0:T(4,128)}, f32[3,64,4,128]{3,2,1,0:T(4,128)}, u32[]{:S(2)}, u32[]{:S(2)}) collective-permute-start(f32[3,64,4,128]{3,2,1,0:T(4,128)} %pad_maximum_fusion.14), channel_id=1, source_target_pairs={{8,0},{16,8},{24,16},{32,24},{40,32},{48,40},{56,48},{64,56},{72,6... | collective-permute-start | bytes 1179656 | tf_op jit(solution)/shard_map/while/body/eval_jaxpr/ppermute | solution.py:20
  110.0 2.8 %collective-permute-done.3 = f32[3,64,4,128]{3,2,1,0:T(4,128)S(1)} collective-permute-done((f32[3,64,4,128]{3,2,1,0:T(4,128)}, f32[3,64,4,128]{3,2,1,0:T(4,128)S(1)}, u32[]{:S(2)}, u32[]{:S(2)}) %collective-permute-start.3) | collective-permute-done | bytes 393248 | tf_op jit(solution)/shard_map/while/body/eval_jaxpr/ppermute | solution.py:20
  112.9 2.6 collective-permute-done.2
  119.4 12.9 %eval_jaxpr.4 = f32[3,64,16,128]{3,2,1,0:T(8,128)S(1)} custom-call(f32[3,68,20,128]{3,2,1,0:T(8,128)S(1)} %select_maximum_fusion.15.xe_ref, f32[3,68,20,128]{3,2,1,0:T(8,128)S(1)} %select_maximum_fusion.16.fe_ref, f32[6,64,16,128]{3,2,1,0:T(8,128)S(1)} %copy-done.3, f32[6,64,16,128]{3,2,1,0:T(8,128)} %get-tuple-element.254.bc_ref, ...), custom_call_target="tpu_custom_call" | custom-call | flops 27525120 | bytes 14139392 | tf_op jit(solution)/shard_map/while/body/eval_jaxpr/pallas_call | solution.py:164
  133.2 1.9 collective-permute-start
  135.1 6.3 %collective-permute-start.1 = (f32[2,3072]{1,0:T(2,128)S(1)}, f32[2,3072]{1,0:T(2,128)S(1)}, u32[]{:S(2)}, u32[]{:S(2)}) collective-permute-start(f32[2,3072]{1,0:T(2,128)S(1)} %get-tuple-element.226), channel_id=1, source_target_pairs={{1,0},{2,1},{3,2},{4,3},{5,4},{6,5},{7,6},{9,8},{10,9},{11,10},{12... | collective-permute-start | bytes 73736 | tf_op jit(solution)/shard_map/while/body/eval_jaxpr/ppermute | solution.py:20
  141.5 1.5 collective-permute-done.1
  145.7 1.9 collective-permute-start.3
  148.5 7.2 %collective-permute-start.2 = (f32[3,64,4,128]{3,2,1,0:T(4,128)}, f32[3,64,4,128]{3,2,1,0:T(4,128)}, u32[]{:S(2)}, u32[]{:S(2)}) collective-permute-start(f32[3,64,4,128]{3,2,1,0:T(4,128)} %pad_maximum_fusion.14), channel_id=1, source_target_pairs={{8,0},{16,8},{24,16},{32,24},{40,32},{48,40},{56,48},{64,56},{72,6... | collective-permute-start | bytes 1179656 | tf_op jit(solution)/shard_map/while/body/eval_jaxpr/ppermute | solution.py:20
  155.8 2.8 %collective-permute-done.3 = f32[3,64,4,128]{3,2,1,0:T(4,128)S(1)} collective-permute-done((f32[3,64,4,128]{3,2,1,0:T(4,128)}, f32[3,64,4,128]{3,2,1,0:T(4,128)S(1)}, u32[]{:S(2)}, u32[]{:S(2)}) %collective-permute-start.3) | collective-permute-done | bytes 393248 | tf_op jit(solution)/shard_map/while/body/eval_jaxpr/ppermute | solution.py:20
  158.8 2.6 collective-permute-done.2
  165.3 12.9 %eval_jaxpr.4 = f32[3,64,16,128]{3,2,1,0:T(8,128)S(1)} custom-call(f32[3,68,20,128]{3,2,1,0:T(8,128)S(1)} %select_maximum_fusion.15.xe_ref, f32[3,68,20,128]{3,2,1,0:T(8,128)S(1)} %select_maximum_fusion.16.fe_ref, f32[6,64,16,128]{3,2,1,0:T(8,128)S(1)} %copy-done.3, f32[6,64,16,128]{3,2,1,0:T(8,128)} %get-tuple-element.254.bc_ref, ...), custom_call_target="tpu_custom_call" | custom-call | flops 27525120 | bytes 14139392 | tf_op jit(solution)/shard_map/while/body/eval_jaxpr/pallas_call | solution.py:164
  179.0 1.9 collective-permute-start
  181.0 6.3 %collective-permute-start.1 = (f32[2,3072]{1,0:T(2,128)S(1)}, f32[2,3072]{1,0:T(2,128)S(1)}, u32[]{:S(2)}, u32[]{:S(2)}) collective-permute-start(f32[2,3072]{1,0:T(2,128)S(1)} %get-tuple-element.226), channel_id=1, source_target_pairs={{1,0},{2,1},{3,2},{4,3},{5,4},{6,5},{7,6},{9,8},{10,9},{11,10},{12... | collective-permute-start | bytes 73736 | tf_op jit(solution)/shard_map/while/body/eval_jaxpr/ppermute | solution.py:20
  187.3 1.5 collective-permute-done.1
  191.5 1.9 collective-permute-start.3
  194.4 7.2 %collective-permute-start.2 = (f32[3,64,4,128]{3,2,1,0:T(4,128)}, f32[3,64,4,128]{3,2,1,0:T(4,128)}, u32[]{:S(2)}, u32[]{:S(2)}) collective-permute-start(f32[3,64,4,128]{3,2,1,0:T(4,128)} %pad_maximum_fusion.14), channel_id=1, source_target_pairs={{8,0},{16,8},{24,16},{32,24},{40,32},{48,40},{56,48},{64,56},{72,6... | collective-permute-start | bytes 1179656 | tf_op jit(solution)/shard_map/while/body/eval_jaxpr/ppermute | solution.py:20
  201.6 2.8 %collective-permute-done.3 = f32[3,64,4,128]{3,2,1,0:T(4,128)S(1)} collective-permute-done((f32[3,64,4,128]{3,2,1,0:T(4,128)}, f32[3,64,4,128]{3,2,1,0:T(4,128)S(1)}, u32[]{:S(2)}, u32[]{:S(2)}) %collective-permute-start.3) | collective-permute-done | bytes 393248 | tf_op jit(solution)/shard_map/while/body/eval_jaxpr/ppermute | solution.py:20
  204.6 2.6 collective-permute-done.2
  211.1 12.9 %eval_jaxpr.4 = f32[3,64,16,128]{3,2,1,0:T(8,128)S(1)} custom-call(f32[3,68,20,128]{3,2,1,0:T(8,128)S(1)} %select_maximum_fusion.15.xe_ref, f32[3,68,20,128]{3,2,1,0:T(8,128)S(1)} %select_maximum_fusion.16.fe_ref, f32[6,64,16,128]{3,2,1,0:T(8,128)S(1)} %copy-done.3, f32[6,64,16,128]{3,2,1,0:T(8,128)} %get-tuple-element.254.bc_ref, ...), custom_call_target="tpu_custom_call" | custom-call | flops 27525120 | bytes 14139392 | tf_op jit(solution)/shard_map/while/body/eval_jaxpr/pallas_call | solution.py:164
  224.9 1.9 collective-permute-start
  226.8 6.3 %collective-permute-start.1 = (f32[2,3072]{1,0:T(2,128)S(1)}, f32[2,3072]{1,0:T(2,128)S(1)}, u32[]{:S(2)}, u32[]{:S(2)}) collective-permute-start(f32[2,3072]{1,0:T(2,128)S(1)} %get-tuple-element.226), channel_id=1, source_target_pairs={{1,0},{2,1},{3,2},{4,3},{5,4},{6,5},{7,6},{9,8},{10,9},{11,10},{12... | collective-permute-start | bytes 73736 | tf_op jit(solution)/shard_map/while/body/eval_jaxpr/ppermute | solution.py:20
  237.4 1.9 collective-permute-start.3
  240.2 7.2 %collective-permute-start.2 = (f32[3,64,4,128]{3,2,1,0:T(4,128)}, f32[3,64,4,128]{3,2,1,0:T(4,128)}, u32[]{:S(2)}, u32[]{:S(2)}) collective-permute-start(f32[3,64,4,128]{3,2,1,0:T(4,128)} %pad_maximum_fusion.14), channel_id=1, source_target_pairs={{8,0},{16,8},{24,16},{32,24},{40,32},{48,40},{56,48},{64,56},{72,6... | collective-permute-start | bytes 1179656 | tf_op jit(solution)/shard_map/while/body/eval_jaxpr/ppermute | solution.py:20
  247.5 2.8 %collective-permute-done.3 = f32[3,64,4,128]{3,2,1,0:T(4,128)S(1)} collective-permute-done((f32[3,64,4,128]{3,2,1,0:T(4,128)}, f32[3,64,4,128]{3,2,1,0:T(4,128)S(1)}, u32[]{:S(2)}, u32[]{:S(2)}) %collective-permute-start.3) | collective-permute-done | bytes 393248 | tf_op jit(solution)/shard_map/while/body/eval_jaxpr/ppermute | solution.py:20
  250.4 2.6 collective-permute-done.2
  257.0 12.9 %eval_jaxpr.4 = f32[3,64,16,128]{3,2,1,0:T(8,128)S(1)} custom-call(f32[3,68,20,128]{3,2,1,0:T(8,128)S(1)} %select_maximum_fusion.15.xe_ref, f32[3,68,20,128]{3,2,1,0:T(8,128)S(1)} %select_maximum_fusion.16.fe_ref, f32[6,64,16,128]{3,2,1,0:T(8,128)S(1)} %copy-done.3, f32[6,64,16,128]{3,2,1,0:T(8,128)} %get-tuple-element.254.bc_ref, ...), custom_call_target="tpu_custom_call" | custom-call | flops 27525120 | bytes 14139392 | tf_op jit(solution)/shard_map/while/body/eval_jaxpr/pallas_call | solution.py:164
  (160 shorter events, 65.2 us)
Async XLA Ops:
  2.8 8.5 %copy-start.13 = (bf16[8,1,128]{2,0,1:T(8,128)(2,1)S(1)}, bf16[8,1,128]{2,0,1:T(8,128)(2,1)}, u32[]{:S(2)}) copy-start(bf16[8,1,128]{2,0,1:T(8,128)(2,1)} %param.17) | copy-start | bytes 6148
  2.8 8.5 %copy-start.14 = (bf16[8,1,16]{2,0,1:T(8,128)(2,1)S(1)}, bf16[8,1,16]{2,0,1:T(8,128)(2,1)}, u32[]{:S(2)}) copy-start(bf16[8,1,16]{2,0,1:T(8,128)(2,1)} %param.16) | copy-start | bytes 772
  2.8 8.6 %copy-start.7 = (bf16[8,64,16,128]{3,2,1,0:T(8,128)(2,1)S(1)}, bf16[8,64,16,128]{3,2,1,0:T(8,128)(2,1)}, u32[]{:S(2)}) copy-start(bf16[8,64,16,128]{3,2,1,0:T(8,128)(2,1)} %param.15) | copy-start | bytes 6291460
  2.8 8.6 %copy-start.15 = (s32[8,1,1]{0,2,1:T(1,128)S(1)}, s32[8,1,1]{0,2,1:T(1,128)}, u32[]{:S(2)}) copy-start(s32[8,1,1]{0,2,1:T(1,128)} %param.19) | copy-start | bytes 100
  3.5 18.3 %collective-permute-start.7 = (f32[2,2048]{1,0:T(2,128)S(1)}, f32[2,2048]{1,0:T(2,128)S(1)}, u32[]{:S(2)}, u32[]{:S(2)}) collective-permute-start(f32[2,2048]{1,0:T(2,128)S(1)} %get-tuple-element.166), channel_id=1, source_target_pairs={{1,0},{2,1},{3,2},{4,3},{5,4},{6,5},{7,6},{9,8},{10,9},{11,10},{12... | collective-permute-start | bytes 49160 | tf_op jit(solution)/shard_map/ppermute | solution.py:20
  8.7 13.1 %collective-permute-start.8 = (f32[2,2048]{1,0:T(2,128)S(1)}, f32[2,2048]{1,0:T(2,128)S(1)}, u32[]{:S(2)}, u32[]{:S(2)}) collective-permute-start(f32[2,2048]{1,0:T(2,128)S(1)} %get-tuple-element.167), channel_id=1, source_target_pairs={{0,1},{1,2},{2,3},{3,4},{4,5},{5,6},{6,7},{8,9},{9,10},{10,11},{11... | collective-permute-start | bytes 49160 | tf_op jit(solution)/shard_map/ppermute | solution.py:20
  11.3 3.8 %copy-start.16 = (s32[8,1,1]{0,2,1:T(1,128)S(1)}, s32[8,1,1]{0,2,1:T(1,128)}, u32[]{:S(2)}) copy-start(s32[8,1,1]{0,2,1:T(1,128)} %param.18) | copy-start | bytes 100
  19.5 32.4 %collective-permute-start.4 = (f32[65,16,128]{2,1,0:T(8,128)S(1)}, f32[65,16,128]{2,1,0:T(8,128)}, u32[]{:S(2)}, u32[]{:S(2)}) collective-permute-start(f32[65,16,128]{2,1,0:T(8,128)S(1)} %pad_maximum_fusion.5), channel_id=1, source_target_pairs={{0,1},{1,2},{2,3},{3,4},{4,5},{5,6},{6,7},{8,9},{9,10},{10,11},{11... | collective-permute-start | bytes 1597448 | tf_op jit(solution)/shard_map/ppermute | solution.py:20
  23.8 15.7 %collective-permute-start.9 = (f32[2,64,4,128]{3,2,1,0:T(4,128)}, f32[2,64,4,128]{3,2,1,0:T(4,128)S(1)}, u32[]{:S(2)}, u32[]{:S(2)}) collective-permute-start(f32[2,64,4,128]{3,2,1,0:T(4,128)} %pad_maximum_fusion.8), channel_id=1, source_target_pairs={{0,8},{8,16},{16,24},{24,32},{32,40},{40,48},{48,56},{56,64},{64,7... | collective-permute-start | bytes 786440 | tf_op jit(solution)/shard_map/ppermute | solution.py:20
  26.5 25.4 %collective-permute-start.5 = (f32[65,16,128]{2,1,0:T(8,128)}, f32[65,16,128]{2,1,0:T(8,128)}, u32[]{:S(2)}, u32[]{:S(2)}) collective-permute-start(f32[65,16,128]{2,1,0:T(8,128)} %pad_maximum_fusion.6), channel_id=1, source_target_pairs={{0,8},{8,16},{16,24},{24,32},{32,40},{40,48},{48,56},{56,64},{64,7... | collective-permute-start | bytes 1597448 | tf_op jit(solution)/shard_map/ppermute | solution.py:20
  31.3 9.4 %collective-permute-start.10 = (f32[2,64,4,128]{3,2,1,0:T(4,128)}, f32[2,64,4,128]{3,2,1,0:T(4,128)}, u32[]{:S(2)}, u32[]{:S(2)}) collective-permute-start(f32[2,64,4,128]{3,2,1,0:T(4,128)} %pad_maximum_fusion.9), channel_id=1, source_target_pairs={{8,0},{16,8},{24,16},{32,24},{40,32},{48,40},{56,48},{64,56},{72,6... | collective-permute-start | bytes 786440 | tf_op jit(solution)/shard_map/ppermute | solution.py:20
  37.4 18.7 %collective-permute-start.6 = (f32[65,16,128]{2,1,0:T(8,128)}, f32[65,16,128]{2,1,0:T(8,128)S(1)}, u32[]{:S(2)}, u32[]{:S(2)}) collective-permute-start(f32[65,16,128]{2,1,0:T(8,128)} %pad_maximum_fusion.7), channel_id=1, source_target_pairs={{0,9},{1,10},{2,11},{3,12},{4,13},{5,14},{6,15},{8,17},{9,18},{10,... | collective-permute-start | bytes 1597448 | tf_op jit(solution)/shard_map/ppermute | solution.py:27
  57.6 4.1 %copy-start.9 = (bf16[64,16,128]{2,1,0:T(8,128)(2,1)}, bf16[64,16,128]{2,1,0:T(8,128)(2,1)S(1)}, u32[]{:S(2)}) copy-start(bf16[64,16,128]{2,1,0:T(8,128)(2,1)S(1)} %get-tuple-element.122) | copy-start | bytes 786436
  57.8 6.2 %collective-permute-start.11 = (f32[2,1024]{1,0:T(2,128)S(1)}, f32[2,1024]{1,0:T(2,128)S(1)}, u32[]{:S(2)}, u32[]{:S(2)}) collective-permute-start(f32[2,1024]{1,0:T(2,128)S(1)} %get-tuple-element.172), channel_id=1, source_target_pairs={{1,0},{2,1},{3,2},{4,3},{5,4},{6,5},{7,6},{9,8},{10,9},{11,10},{12... | collective-permute-start | bytes 24584 | tf_op jit(solution)/shard_map/ppermute | solution.py:20
  61.7 7.7 %collective-permute-start.12 = (f32[2,1024]{1,0:T(2,128)S(1)}, f32[2,1024]{1,0:T(2,128)S(1)}, u32[]{:S(2)}, u32[]{:S(2)}) collective-permute-start(f32[2,1024]{1,0:T(2,128)S(1)} %get-tuple-element.173), channel_id=1, source_target_pairs={{0,1},{1,2},{2,3},{3,4},{4,5},{5,6},{6,7},{8,9},{9,10},{10,11},{11... | collective-permute-start | bytes 24584 | tf_op jit(solution)/shard_map/ppermute | solution.py:20
  70.1 9.9 %collective-permute-start.13 = (f32[1,64,4,128]{3,2,1,0:T(4,128)S(1)}, f32[1,64,4,128]{3,2,1,0:T(4,128)S(1)}, u32[]{:S(2)}, u32[]{:S(2)}) collective-permute-start(f32[1,64,4,128]{3,2,1,0:T(4,128)S(1)} %pad_maximum_fusion.10), channel_id=1, source_target_pairs={{0,8},{8,16},{16,24},{24,32},{32,40},{40,48},{48,56},{56,64},{64,7... | collective-permute-start | bytes 393224 | tf_op jit(solution)/shard_map/ppermute | solution.py:20
  72.4 10.3 %copy-start.2 = (f32[6,64,16,128]{3,2,1,0:T(8,128)}, f32[6,64,16,128]{3,2,1,0:T(8,128)S(1)}, u32[]{:S(2)}) copy-start(f32[6,64,16,128]{3,2,1,0:T(8,128)S(1)} %fusion.35) | copy-start | bytes 9437188
  72.5 9.8 %collective-permute-start.14 = (f32[1,64,4,128]{3,2,1,0:T(4,128)S(1)}, f32[1,64,4,128]{3,2,1,0:T(4,128)S(1)}, u32[]{:S(2)}, u32[]{:S(2)}) collective-permute-start(f32[1,64,4,128]{3,2,1,0:T(4,128)S(1)} %pad_maximum_fusion.11), channel_id=1, source_target_pairs={{8,0},{16,8},{24,16},{32,24},{40,32},{48,40},{56,48},{64,56},{72,6... | collective-permute-start | bytes 393224 | tf_op jit(solution)/shard_map/ppermute | solution.py:20
  84.8 2.0 copy-start.1
  84.8 2.0 copy-start.11
  87.7 8.0 %collective-permute-start = (f32[2,3072]{1,0:T(2,128)S(1)}, f32[2,3072]{1,0:T(2,128)S(1)}, u32[]{:S(2)}, u32[]{:S(2)}) collective-permute-start(f32[2,3072]{1,0:T(2,128)S(1)} %get-tuple-element.225), channel_id=1, source_target_pairs={{0,1},{1,2},{2,3},{3,4},{4,5},{5,6},{6,7},{8,9},{9,10},{10,11},{11... | collective-permute-start | bytes 73736 | tf_op jit(solution)/shard_map/while/body/eval_jaxpr/ppermute | solution.py:20
  89.6 7.5 %collective-permute-start.1 = (f32[2,3072]{1,0:T(2,128)S(1)}, f32[2,3072]{1,0:T(2,128)S(1)}, u32[]{:S(2)}, u32[]{:S(2)}) collective-permute-start(f32[2,3072]{1,0:T(2,128)S(1)} %get-tuple-element.226), channel_id=1, source_target_pairs={{1,0},{2,1},{3,2},{4,3},{5,4},{6,5},{7,6},{9,8},{10,9},{11,10},{12... | collective-permute-start | bytes 73736 | tf_op jit(solution)/shard_map/while/body/eval_jaxpr/ppermute | solution.py:20
  99.9 12.9 %collective-permute-start.3 = (f32[3,64,4,128]{3,2,1,0:T(4,128)}, f32[3,64,4,128]{3,2,1,0:T(4,128)S(1)}, u32[]{:S(2)}, u32[]{:S(2)}) collective-permute-start(f32[3,64,4,128]{3,2,1,0:T(4,128)} %pad_maximum_fusion.15), channel_id=1, source_target_pairs={{0,8},{8,16},{16,24},{24,32},{32,40},{40,48},{48,56},{56,64},{64,7... | collective-permute-start | bytes 1179656 | tf_op jit(solution)/shard_map/while/body/eval_jaxpr/ppermute | solution.py:20
  102.7 12.8 %collective-permute-start.2 = (f32[3,64,4,128]{3,2,1,0:T(4,128)}, f32[3,64,4,128]{3,2,1,0:T(4,128)}, u32[]{:S(2)}, u32[]{:S(2)}) collective-permute-start(f32[3,64,4,128]{3,2,1,0:T(4,128)} %pad_maximum_fusion.14), channel_id=1, source_target_pairs={{8,0},{16,8},{24,16},{32,24},{40,32},{48,40},{56,48},{64,56},{72,6... | collective-permute-start | bytes 1179656 | tf_op jit(solution)/shard_map/while/body/eval_jaxpr/ppermute | solution.py:20
  116.9 1.4 copy-start.4
  117.3 2.1 copy-start.3
  117.3 2.2 copy-start.5
  133.2 8.3 %collective-permute-start = (f32[2,3072]{1,0:T(2,128)S(1)}, f32[2,3072]{1,0:T(2,128)S(1)}, u32[]{:S(2)}, u32[]{:S(2)}) collective-permute-start(f32[2,3072]{1,0:T(2,128)S(1)} %get-tuple-element.225), channel_id=1, source_target_pairs={{0,1},{1,2},{2,3},{3,4},{4,5},{5,6},{6,7},{8,9},{9,10},{10,11},{11... | collective-permute-start | bytes 73736 | tf_op jit(solution)/shard_map/while/body/eval_jaxpr/ppermute | solution.py:20
  135.1 7.8 %collective-permute-start.1 = (f32[2,3072]{1,0:T(2,128)S(1)}, f32[2,3072]{1,0:T(2,128)S(1)}, u32[]{:S(2)}, u32[]{:S(2)}) collective-permute-start(f32[2,3072]{1,0:T(2,128)S(1)} %get-tuple-element.226), channel_id=1, source_target_pairs={{1,0},{2,1},{3,2},{4,3},{5,4},{6,5},{7,6},{9,8},{10,9},{11,10},{12... | collective-permute-start | bytes 73736 | tf_op jit(solution)/shard_map/while/body/eval_jaxpr/ppermute | solution.py:20
  145.7 12.9 %collective-permute-start.3 = (f32[3,64,4,128]{3,2,1,0:T(4,128)}, f32[3,64,4,128]{3,2,1,0:T(4,128)S(1)}, u32[]{:S(2)}, u32[]{:S(2)}) collective-permute-start(f32[3,64,4,128]{3,2,1,0:T(4,128)} %pad_maximum_fusion.15), channel_id=1, source_target_pairs={{0,8},{8,16},{16,24},{24,32},{32,40},{40,48},{48,56},{56,64},{64,7... | collective-permute-start | bytes 1179656 | tf_op jit(solution)/shard_map/while/body/eval_jaxpr/ppermute | solution.py:20
  148.5 12.8 %collective-permute-start.2 = (f32[3,64,4,128]{3,2,1,0:T(4,128)}, f32[3,64,4,128]{3,2,1,0:T(4,128)}, u32[]{:S(2)}, u32[]{:S(2)}) collective-permute-start(f32[3,64,4,128]{3,2,1,0:T(4,128)} %pad_maximum_fusion.14), channel_id=1, source_target_pairs={{8,0},{16,8},{24,16},{32,24},{40,32},{48,40},{56,48},{64,56},{72,6... | collective-permute-start | bytes 1179656 | tf_op jit(solution)/shard_map/while/body/eval_jaxpr/ppermute | solution.py:20
  162.7 1.4 copy-start.4
  163.1 2.1 copy-start.3
  163.1 2.2 copy-start.5
  179.0 8.3 %collective-permute-start = (f32[2,3072]{1,0:T(2,128)S(1)}, f32[2,3072]{1,0:T(2,128)S(1)}, u32[]{:S(2)}, u32[]{:S(2)}) collective-permute-start(f32[2,3072]{1,0:T(2,128)S(1)} %get-tuple-element.225), channel_id=1, source_target_pairs={{0,1},{1,2},{2,3},{3,4},{4,5},{5,6},{6,7},{8,9},{9,10},{10,11},{11... | collective-permute-start | bytes 73736 | tf_op jit(solution)/shard_map/while/body/eval_jaxpr/ppermute | solution.py:20
  181.0 7.8 %collective-permute-start.1 = (f32[2,3072]{1,0:T(2,128)S(1)}, f32[2,3072]{1,0:T(2,128)S(1)}, u32[]{:S(2)}, u32[]{:S(2)}) collective-permute-start(f32[2,3072]{1,0:T(2,128)S(1)} %get-tuple-element.226), channel_id=1, source_target_pairs={{1,0},{2,1},{3,2},{4,3},{5,4},{6,5},{7,6},{9,8},{10,9},{11,10},{12... | collective-permute-start | bytes 73736 | tf_op jit(solution)/shard_map/while/body/eval_jaxpr/ppermute | solution.py:20
  191.5 12.9 %collective-permute-start.3 = (f32[3,64,4,128]{3,2,1,0:T(4,128)}, f32[3,64,4,128]{3,2,1,0:T(4,128)S(1)}, u32[]{:S(2)}, u32[]{:S(2)}) collective-permute-start(f32[3,64,4,128]{3,2,1,0:T(4,128)} %pad_maximum_fusion.15), channel_id=1, source_target_pairs={{0,8},{8,16},{16,24},{24,32},{32,40},{40,48},{48,56},{56,64},{64,7... | collective-permute-start | bytes 1179656 | tf_op jit(solution)/shard_map/while/body/eval_jaxpr/ppermute | solution.py:20
  194.4 12.8 %collective-permute-start.2 = (f32[3,64,4,128]{3,2,1,0:T(4,128)}, f32[3,64,4,128]{3,2,1,0:T(4,128)}, u32[]{:S(2)}, u32[]{:S(2)}) collective-permute-start(f32[3,64,4,128]{3,2,1,0:T(4,128)} %pad_maximum_fusion.14), channel_id=1, source_target_pairs={{8,0},{16,8},{24,16},{32,24},{40,32},{48,40},{56,48},{64,56},{72,6... | collective-permute-start | bytes 1179656 | tf_op jit(solution)/shard_map/while/body/eval_jaxpr/ppermute | solution.py:20
  208.6 1.4 copy-start.4
  209.0 2.1 copy-start.3
  209.0 2.2 copy-start.5
  224.9 8.3 %collective-permute-start = (f32[2,3072]{1,0:T(2,128)S(1)}, f32[2,3072]{1,0:T(2,128)S(1)}, u32[]{:S(2)}, u32[]{:S(2)}) collective-permute-start(f32[2,3072]{1,0:T(2,128)S(1)} %get-tuple-element.225), channel_id=1, source_target_pairs={{0,1},{1,2},{2,3},{3,4},{4,5},{5,6},{6,7},{8,9},{9,10},{10,11},{11... | collective-permute-start | bytes 73736 | tf_op jit(solution)/shard_map/while/body/eval_jaxpr/ppermute | solution.py:20
  226.8 7.8 %collective-permute-start.1 = (f32[2,3072]{1,0:T(2,128)S(1)}, f32[2,3072]{1,0:T(2,128)S(1)}, u32[]{:S(2)}, u32[]{:S(2)}) collective-permute-start(f32[2,3072]{1,0:T(2,128)S(1)} %get-tuple-element.226), channel_id=1, source_target_pairs={{1,0},{2,1},{3,2},{4,3},{5,4},{6,5},{7,6},{9,8},{10,9},{11,10},{12... | collective-permute-start | bytes 73736 | tf_op jit(solution)/shard_map/while/body/eval_jaxpr/ppermute | solution.py:20
  237.4 12.9 %collective-permute-start.3 = (f32[3,64,4,128]{3,2,1,0:T(4,128)}, f32[3,64,4,128]{3,2,1,0:T(4,128)S(1)}, u32[]{:S(2)}, u32[]{:S(2)}) collective-permute-start(f32[3,64,4,128]{3,2,1,0:T(4,128)} %pad_maximum_fusion.15), channel_id=1, source_target_pairs={{0,8},{8,16},{16,24},{24,32},{32,40},{40,48},{48,56},{56,64},{64,7... | collective-permute-start | bytes 1179656 | tf_op jit(solution)/shard_map/while/body/eval_jaxpr/ppermute | solution.py:20
  240.2 12.8 %collective-permute-start.2 = (f32[3,64,4,128]{3,2,1,0:T(4,128)}, f32[3,64,4,128]{3,2,1,0:T(4,128)}, u32[]{:S(2)}, u32[]{:S(2)}) collective-permute-start(f32[3,64,4,128]{3,2,1,0:T(4,128)} %pad_maximum_fusion.14), channel_id=1, source_target_pairs={{8,0},{16,8},{24,16},{32,24},{40,32},{48,40},{56,48},{64,56},{72,6... | collective-permute-start | bytes 1179656 | tf_op jit(solution)/shard_map/while/body/eval_jaxpr/ppermute | solution.py:20
  254.4 1.4 copy-start.4
  254.8 2.1 copy-start.3
  254.8 2.2 copy-start.5
  (5 other events, 5.3 us)
where the time goes:
time: 275 us; the launch traced here: 271 us
  starting transfers between devices  107 us (39%)
  Pallas kernels  51.5 us (19%)
  waiting for transfers between devices  40.6 us (15%)
  local copies, waits for them, and re-layouts  26.6 us (10%)
  other arithmetic  23.8 us (9%)
  matrix products  19.2 us (7%)
    ppermute x26, starting transfers between devices, shifted_in(): return lax.ppermute(block, axis, route)  105 us
    pallas_call x4, Pallas kernels, relax_call(): pl.pallas_call(relax_kernel, out_shape=out_shape, grid=(depth // chunk,),...  51.5 us
    ppermute x26, waiting for transfers between devices, shifted_in(): return lax.ppermute(block, axis, route)  36.4 us
    unnamed x33, local copies, waits for them, and re-layouts  8.33 us
    dot_general x6, matrix products, halo(): jnp.einsum('kr,ky->ry', arrived, pick, precision=EXACT).reshape(v.shape)  7.28 us
    while x24, local copies, waits for them, and re-layouts  7.18 us
  transfers between devices with their start and end apart: 27, of which 17 were waited for; matrix products, arithmetic and copies ran while one was open for 11% of the time, Pallas kernels for 0%

commit v1 on v0

--- a/solution.py
+++ b/solution.py
@@ -32,22 +32,59 @@
     return (lax.broadcasted_iota(jnp.int32, (4, wide_y), 1) == lanes[:, None]).astype(jnp.float32)
 
 
+def exact_pick(equation, values, pick):
+    high = lax.reduce_precision(values, exponent_bits=8, mantissa_bits=7)
+    rest = values - high
+    middle = lax.reduce_precision(rest, exponent_bits=8, mantissa_bits=7)
+    low = rest - middle
+    ones = pick.astype(jnp.bfloat16)
+
+    def part(piece):
+        return jnp.einsum(
+            equation, ones, piece.astype(jnp.bfloat16), preferred_element_type=jnp.float32
+        )
+
+    return (part(high) + part(middle)) + part(low)
+
+
 def halo(v):
     chans, depth, wide_x, wide_y = v.shape
     pick = edge_lanes(wide_y)
     rows = v.reshape(chans * depth * wide_x, wide_y)
-    strips = jnp.einsum("ky,ry->kr", pick, rows, precision=EXACT)
-    y_high = shifted_in(strips[:2], "gy", -1)
-    y_low = shifted_in(strips[2:], "gy", 1)
-    arrived = jnp.concatenate([y_high, y_low], axis=0)
-    wrapped = jnp.einsum("kr,ky->ry", arrived, pick, precision=EXACT).reshape(v.shape)
-    upward = jnp.concatenate([v[:, :, wide_x - 2 :], wrapped[:, :, wide_x - 2 :]], axis=2)
-    downward = jnp.concatenate([v[:, :, :2], wrapped[:, :, :2]], axis=2)
-    x_low = shifted_in(upward, "gx", 1)
-    x_high = shifted_in(downward, "gx", -1)
+    strips = exact_pick("ky,ry->kr", rows, pick).reshape(4, chans, depth, wide_x)
+    first = strips[:2]
+    last = strips[2:]
+    nx = lax.axis_size("gx")
+    ny = lax.axis_size("gy")
+
+    def corner(block, step_x, step_y):
+        route = []
+        for i in range(nx):
+            for j in range(ny):
+                if 0 <= i + step_x < nx and 0 <= j + step_y < ny:
+                    route.append((i * ny + j, (i + step_x) * ny + j + step_y))
+        return lax.ppermute(block, ("gx", "gy"), route)
+
+    y_high = shifted_in(first, "gy", -1)
+    y_low = shifted_in(last, "gy", 1)
+    x_low = shifted_in(v[:, :, wide_x - 2 :], "gx", 1)
+    x_high = shifted_in(v[:, :, :2], "gx", -1)
+    low_high = corner(first[..., wide_x - 2 :], 1, -1)
+    low_low = corner(last[..., wide_x - 2 :], 1, 1)
+    high_high = corner(first[..., :2], -1, -1)
+    high_low = corner(last[..., :2], -1, 1)
+    arrived = jnp.concatenate(
+        [
+            jnp.concatenate([low_high, y_high, high_high], axis=-1),
+            jnp.concatenate([low_low, y_low, high_low], axis=-1),
+        ],
+        axis=0,
+    )
+    tall = wide_x + 4
+    wrapped = exact_pick("ky,kr->ry", arrived.reshape(4, chans * depth * tall), pick)
     z_pad = ((0, 0), (2, 2), (0, 0), (0, 0))
-    xe = jnp.pad(jnp.concatenate([x_low[:, :, :2], v, x_high[:, :, :2]], axis=2), z_pad)
-    fe = jnp.pad(jnp.concatenate([x_low[:, :, 2:], wrapped, x_high[:, :, 2:]], axis=2), z_pad)
+    xe = jnp.pad(jnp.concatenate([x_low, v, x_high], axis=2), z_pad)
+    fe = jnp.pad(wrapped.reshape(chans, depth, tall, wide_y), z_pad)
     return xe, fe
 
 

time: 275 us -> 378 us (1.37)
  starting transfers between devices: 107 us -> 217 us
  waiting for transfers between devices: 40.6 us -> 15.6 us
  local copies, waits for them, and re-layouts: 26.6 us -> 38.9 us
  matrix products: 19.2 us -> 26.8 us
    ppermute x0 -> x24, starting transfers between devices: none -> 116 us  [corner(): return lax.ppermute(block, ('gx', 'gy'), route)]
    ppermute x26, waiting for transfers between devices: 36.4 us -> 7.66 us  [shifted_in(): return lax.ppermute(block, axis, route)]
    reshape x0 -> x12, local copies, waits for them, and re-layouts: none -> 9.04 us  [the longest x6 7.67 us: halo(): fe = jnp.pad(wrapped.reshape(chans, depth, tall, wide_y), z_pad)]
    pad x0 -> x4, local copies, waits for them, and re-layouts: none -> 7.91 us  [halo(): fe = jnp.pad(wrapped.reshape(chans, depth, tall, wide_y), z_pad)]
    dot_general x12 -> x36, matrix products: 11.3 us -> 18.2 us  [part(): jnp.einsum(equation, ones, piece.astype(jnp.bfloat16), preferred_element_...]
    while x24 -> x40, local copies, waits for them, and re-layouts: 7.18 us -> 0.48 us
    ppermute x26, starting transfers between devices: 105 us -> 99 us  [shifted_in(): return lax.ppermute(block, axis, route)]
    concatenate x24 -> x12, other arithmetic: 13.1 us -> 8.42 us  [the longest x6 6.77 us: halo(): xe = jnp.pad(jnp.concatenate([x_low, v, x_high], axis=2), z_pad)]
  transfers between devices with their start and end apart: 27 -> 51, of which waited for: 17 -> 5; matrix products, arithmetic and copies ran while one was open for 11% -> 17% of each run, Pallas kernels for 0% -> 0%
where the time goes in v1:
time: 378 us; the launch traced here: 374 us
  starting transfers between devices  217 us (57%)
  Pallas kernels  48.6 us (13%)
  local copies, waits for them, and re-layouts  38.9 us (10%)
  matrix products  26.8 us (7%)
  other arithmetic  24.1 us (6%)
  waiting for transfers between devices  15.6 us (4%)
    ppermute x24, starting transfers between devices, corner(): return lax.ppermute(block, ('gx', 'gy'), route)  116 us
    ppermute x26, starting transfers between devices, shifted_in(): return lax.ppermute(block, axis, route)  99 us
    pallas_call x4, Pallas kernels, relax_call(): pl.pallas_call(relax_kernel, out_shape=out_shape, grid=(depth // chunk,),...  48.6 us
    dot_general x36, matrix products, part(): jnp.einsum(equation, ones, piece.astype(jnp.bfloat16), preferred_element_...  18.2 us
    pad x4, local copies, waits for them, and re-layouts, halo(): fe = jnp.pad(wrapped.reshape(chans, depth, tall, wide_y), z_pad)  7.91 us
    ppermute x1, waiting for transfers between devices, diagonal_in(): return lax.ppermute(block, ('gx', 'gy'), route)  7.87 us
    reshape x6, local copies, waits for them, and re-layouts, halo(): fe = jnp.pad(wrapped.reshape(chans, depth, tall, wide_y), z_pad)  7.67 us
    ppermute x26, waiting for transfers between devices, shifted_in(): return lax.ppermute(block, axis, route)  7.66 us
  transfers between devices with their start and end apart: 51, of which 5 were waited for; matrix products, arithmetic and copies ran while one was open for 17% of the time, Pallas kernels for 0%

profile of v1, /device:TPU:6, one launch (start us, length us, event | category | flops | bytes accessed | tf_op | source)
XLA Modules:
  0.0 374.0 jit_solution(4852137414083907923)
XLA Ops:
  4.4 5.2 %collective-permute-start.12 = (f32[2,2,64,16]{3,2,1,0:T(8,128)S(1)}, f32[2,2,64,16]{3,2,1,0:T(8,128)}, u32[]{:S(2)}, u32[]{:S(2)}) collective-permute-start(f32[2,2,64,16]{3,2,1,0:T(8,128)S(1)} %slice.233), channel_id=1, source_target_pairs={{1,0},{2,1},{3,2},{4,3},{5,4},{6,5},{7,6},{9,8},{10,9},{11,10},{12... | collective-permute-start | bytes 49160 | tf_op jit(solution)/shard_map/ppermute | solution.py:20
  12.2 7.0 %collective-permute-start.13 = (f32[2,2,64,2]{3,2,1,0:T(8,128)}, f32[2,2,64,2]{3,2,1,0:T(8,128)}, u32[]{:S(2)}, u32[]{:S(2)}) collective-permute-start(f32[2,2,64,2]{3,2,1,0:T(8,128)} %get-tuple-element.160), channel_id=1, source_target_pairs={{9,0},{10,1},{11,2},{12,3},{13,4},{14,5},{15,6},{17,8},{18,9},{19,... | collective-permute-start | bytes 6152 | tf_op jit(solution)/shard_map/ppermute | solution.py:66
  19.3 2.9 collective-permute-start.15
  25.1 4.4 %fusion.12 = f32[8,64,16,256]{3,2,0,1:T(8,128)S(1)} fusion(s32[8]{0:T(128)} %bitcast.159, bf16[8,64,16,128]{3,2,1,0:T(8,128)(2,1)S(1)} %copy-done.10, f32[8,128]{1,0:T(8,128)S(1)} %bitcast_convert_fusion, f32[8,16]{1,0:T(8,128)S(1)} %convert_multiply_fusion), kind=kOutput, calls=%fused_computation.30 | convolution fusion | flops 3224895488 | bytes 10490400 | tf_op jit(solution)/shard_map/szxy,syY->szxY/dot_general | solution.py:123
  29.5 3.3 convolution_bitcast_fusion
  38.6 8.3 %collective-permute-start.16 = (f32[2,2,64,2]{3,2,1,0:T(8,128)}, f32[2,2,64,2]{3,2,1,0:T(8,128)S(1)}, u32[]{:S(2)}, u32[]{:S(2)}) collective-permute-start(f32[2,2,64,2]{3,2,1,0:T(8,128)} %get-tuple-element.162), channel_id=1, source_target_pairs={{8,1},{9,2},{10,3},{11,4},{12,5},{13,6},{14,7},{16,9},{17,10},{18,... | collective-permute-start | bytes 6152 | tf_op jit(solution)/shard_map/ppermute | solution.py:66
  49.7 1.9 collective-permute-start.9
  51.6 1.9 collective-permute-start.17
  53.5 8.0 %collective-permute-start.18 = (f32[2,64,2,128]{3,2,1,0:T(2,128)S(1)}, f32[2,64,2,128]{3,2,1,0:T(2,128)S(1)}, u32[]{:S(2)}, u32[]{:S(2)}) collective-permute-start(f32[2,64,2,128]{3,2,1,0:T(2,128)S(1)} %get-tuple-element.148), channel_id=1, source_target_pairs={{8,0},{16,8},{24,16},{32,24},{40,32},{48,40},{56,48},{64,56},{72,6... | collective-permute-start | bytes 393224 | tf_op jit(solution)/shard_map/ppermute | solution.py:20
  67.8 2.1 collective-permute-start.10
  75.9 7.9 %collective-permute-done.10 = f32[65,16,128]{2,1,0:T(8,128)S(1)} collective-permute-done((f32[65,16,128]{2,1,0:T(8,128)S(1)}, f32[65,16,128]{2,1,0:T(8,128)S(1)}, u32[]{:S(2)}, u32[]{:S(2)}) %collective-permute-start.10) | collective-permute-done | bytes 532512 | tf_op jit(solution)/shard_map/ppermute | solution.py:27
  86.8 4.3 %collective-permute-start.20 = (f32[2,1,64,16]{3,2,0,1:T(8,128)S(1)}, f32[2,1,64,16]{3,2,0,1:T(8,128)S(1)}, u32[]{:S(2)}, u32[]{:S(2)}) collective-permute-start(f32[2,1,64,16]{3,2,0,1:T(8,128)S(1)} %slice.260), channel_id=1, source_target_pairs={{1,0},{2,1},{3,2},{4,3},{5,4},{6,5},{7,6},{9,8},{10,9},{11,10},{12... | collective-permute-start | bytes 24584 | tf_op jit(solution)/shard_map/ppermute | solution.py:20
  95.1 8.7 %collective-permute-start.21 = (f32[2,1,64,2]{3,2,0,1:T(8,128)S(1)}, f32[2,1,64,2]{3,2,0,1:T(8,128)S(1)}, u32[]{:S(2)}, u32[]{:S(2)}) collective-permute-start(f32[2,1,64,2]{3,2,0,1:T(8,128)S(1)} %get-tuple-element.164), channel_id=1, source_target_pairs={{9,0},{10,1},{11,2},{12,3},{13,4},{14,5},{15,6},{17,8},{18,9},{19,... | collective-permute-start | bytes 3080 | tf_op jit(solution)/shard_map/ppermute | solution.py:66
  105.8 7.6 %collective-permute-start.24 = (f32[2,1,64,2]{3,2,0,1:T(8,128)S(1)}, f32[2,1,64,2]{3,2,0,1:T(8,128)S(1)}, u32[]{:S(2)}, u32[]{:S(2)}) collective-permute-start(f32[2,1,64,2]{3,2,0,1:T(8,128)S(1)} %get-tuple-element.166), channel_id=1, source_target_pairs={{8,1},{9,2},{10,3},{11,4},{12,5},{13,6},{14,7},{16,9},{17,10},{18,... | collective-permute-start | bytes 3080 | tf_op jit(solution)/shard_map/ppermute | solution.py:66
  115.6 7.5 %collective-permute-start.26 = (f32[1,64,2,128]{3,2,1,0:T(2,128)S(1)}, f32[1,64,2,128]{3,2,1,0:T(2,128)S(1)}, u32[]{:S(2)}, u32[]{:S(2)}) collective-permute-start(f32[1,64,2,128]{3,2,1,0:T(2,128)S(1)} %get-tuple-element.155), channel_id=1, source_target_pairs={{8,0},{16,8},{24,16},{32,24},{40,32},{48,40},{56,48},{64,56},{72,6... | collective-permute-start | bytes 196616 | tf_op jit(solution)/shard_map/ppermute | solution.py:20
  129.1 243.7 %while.13 = (s32[]{:T(128)}, f32[3,64,16,128]{3,2,1,0:T(8,128)S(1)}, f32[6,64,16,128]{3,2,1,0:T(8,128)}, f32[6,64,16,128]{3,2,1,0:T(8,128)}, f32[64,16,128]{2,1,...) while((s32[]{:T(128)}, ...), condition=%wide.region_1.2_spmd.clone, body=%wide.region_0.1_spmd.sunk.clone.sunk | while | flops 56951808 | bytes 79852176 | solution.py:275
  132.7 6.1 %collective-permute-start.2 = (f32[2,3,64,2]{3,2,1,0:T(8,128)S(1)}, f32[2,3,64,2]{3,2,1,0:T(8,128)S(1)}, u32[]{:S(2)}, u32[]{:S(2)}) collective-permute-start(f32[2,3,64,2]{3,2,1,0:T(8,128)S(1)} %get-tuple-element.231), channel_id=1, source_target_pairs={{8,1},{9,2},{10,3},{11,4},{12,5},{13,6},{14,7},{16,9},{17,10},{18,... | collective-permute-start | bytes 9224 | tf_op jit(solution)/shard_map/while/body/eval_jaxpr/ppermute | solution.py:66
  138.9 1.9 collective-permute-start.4
  140.9 4.9 %collective-permute-start.6 = (f32[2,3,64,16]{3,2,1,0:T(8,128)S(1)}, f32[2,3,64,16]{3,2,1,0:T(8,128)S(1)}, u32[]{:S(2)}, u32[]{:S(2)}) collective-permute-start(f32[2,3,64,16]{3,2,1,0:T(8,128)S(1)} %slice.525), channel_id=1, source_target_pairs={{1,0},{2,1},{3,2},{4,3},{5,4},{6,5},{7,6},{9,8},{10,9},{11,10},{12... | collective-permute-start | bytes 73736 | tf_op jit(solution)/shard_map/while/body/eval_jaxpr/ppermute | solution.py:20
  146.6 7.6 %collective-permute-start.5 = (f32[2,3,64,2]{3,2,1,0:T(8,128)}, f32[2,3,64,2]{3,2,1,0:T(8,128)S(1)}, u32[]{:S(2)}, u32[]{:S(2)}) collective-permute-start(f32[2,3,64,2]{3,2,1,0:T(8,128)} %get-tuple-element.234), channel_id=1, source_target_pairs={{9,0},{10,1},{11,2},{12,3},{13,4},{14,5},{15,6},{17,8},{18,9},{19,... | collective-permute-start | bytes 9224 | tf_op jit(solution)/shard_map/while/body/eval_jaxpr/ppermute | solution.py:66
  157.2 8.7 %collective-permute-start = (f32[3,64,2,128]{3,2,1,0:T(2,128)}, f32[3,64,2,128]{3,2,1,0:T(2,128)}, u32[]{:S(2)}, u32[]{:S(2)}) collective-permute-start(f32[3,64,2,128]{3,2,1,0:T(2,128)} %get-tuple-element.225), channel_id=1, source_target_pairs={{8,0},{16,8},{24,16},{32,24},{40,32},{48,40},{56,48},{64,56},{72,6... | collective-permute-start | bytes 589832 | tf_op jit(solution)/shard_map/while/body/eval_jaxpr/ppermute | solution.py:20
  166.0 1.9 collective-permute-start.1
  173.0 2.0 pad.168.fe_ref
  178.4 12.2 %eval_jaxpr.4 = f32[3,64,16,128]{3,2,1,0:T(8,128)S(1)} custom-call(f32[3,68,20,128]{3,2,1,0:T(8,128)S(1)} %select_maximum_fusion.8.xe_ref, f32[3,68,20,128]{3,2,1,0:T(8,128)S(1)} %pad.168.fe_ref, f32[6,64,16,128]{3,2,1,0:T(8,128)S(1)} %copy-done.3, f32[6,64,16,128]{3,2,1,0:T(8,128)S(1)} %copy-done.5, f32[64,16,128]{2,1,0:T(8,128)S(1)} %copy-done.8, ...), custom_call_target="tpu_custom_call" | custom-call | flops 27525120 | bytes 14139392 | tf_op jit(solution)/shard_map/while/body/eval_jaxpr/pallas_call | solution.py:201
  194.2 6.6 %collective-permute-start.2 = (f32[2,3,64,2]{3,2,1,0:T(8,128)S(1)}, f32[2,3,64,2]{3,2,1,0:T(8,128)S(1)}, u32[]{:S(2)}, u32[]{:S(2)}) collective-permute-start(f32[2,3,64,2]{3,2,1,0:T(8,128)S(1)} %get-tuple-element.231), channel_id=1, source_target_pairs={{8,1},{9,2},{10,3},{11,4},{12,5},{13,6},{14,7},{16,9},{17,10},{18,... | collective-permute-start | bytes 9224 | tf_op jit(solution)/shard_map/while/body/eval_jaxpr/ppermute | solution.py:66
  200.8 1.9 collective-permute-start.4
  202.9 3.7 collective-permute-start.6
  207.4 7.6 %collective-permute-start.5 = (f32[2,3,64,2]{3,2,1,0:T(8,128)}, f32[2,3,64,2]{3,2,1,0:T(8,128)S(1)}, u32[]{:S(2)}, u32[]{:S(2)}) collective-permute-start(f32[2,3,64,2]{3,2,1,0:T(8,128)} %get-tuple-element.234), channel_id=1, source_target_pairs={{9,0},{10,1},{11,2},{12,3},{13,4},{14,5},{15,6},{17,8},{18,9},{19,... | collective-permute-start | bytes 9224 | tf_op jit(solution)/shard_map/while/body/eval_jaxpr/ppermute | solution.py:66
  217.9 8.7 %collective-permute-start = (f32[3,64,2,128]{3,2,1,0:T(2,128)}, f32[3,64,2,128]{3,2,1,0:T(2,128)}, u32[]{:S(2)}, u32[]{:S(2)}) collective-permute-start(f32[3,64,2,128]{3,2,1,0:T(2,128)} %get-tuple-element.225), channel_id=1, source_target_pairs={{8,0},{16,8},{24,16},{32,24},{40,32},{48,40},{56,48},{64,56},{72,6... | collective-permute-start | bytes 589832 | tf_op jit(solution)/shard_map/while/body/eval_jaxpr/ppermute | solution.py:20
  226.8 1.9 collective-permute-start.1
  233.8 2.0 pad.168.fe_ref
  239.1 12.2 %eval_jaxpr.4 = f32[3,64,16,128]{3,2,1,0:T(8,128)S(1)} custom-call(f32[3,68,20,128]{3,2,1,0:T(8,128)S(1)} %select_maximum_fusion.8.xe_ref, f32[3,68,20,128]{3,2,1,0:T(8,128)S(1)} %pad.168.fe_ref, f32[6,64,16,128]{3,2,1,0:T(8,128)S(1)} %copy-done.3, f32[6,64,16,128]{3,2,1,0:T(8,128)S(1)} %copy-done.5, f32[64,16,128]{2,1,0:T(8,128)S(1)} %copy-done.8, ...), custom_call_target="tpu_custom_call" | custom-call | flops 27525120 | bytes 14139392 | tf_op jit(solution)/shard_map/while/body/eval_jaxpr/pallas_call | solution.py:201
  255.0 7.8 %collective-permute-start.2 = (f32[2,3,64,2]{3,2,1,0:T(8,128)S(1)}, f32[2,3,64,2]{3,2,1,0:T(8,128)S(1)}, u32[]{:S(2)}, u32[]{:S(2)}) collective-permute-start(f32[2,3,64,2]{3,2,1,0:T(8,128)S(1)} %get-tuple-element.231), channel_id=1, source_target_pairs={{8,1},{9,2},{10,3},{11,4},{12,5},{13,6},{14,7},{16,9},{17,10},{18,... | collective-permute-start | bytes 9224 | tf_op jit(solution)/shard_map/while/body/eval_jaxpr/ppermute | solution.py:66
  262.8 1.9 collective-permute-start.4
  264.9 2.5 collective-permute-start.6
  268.1 8.5 %collective-permute-start.5 = (f32[2,3,64,2]{3,2,1,0:T(8,128)}, f32[2,3,64,2]{3,2,1,0:T(8,128)S(1)}, u32[]{:S(2)}, u32[]{:S(2)}) collective-permute-start(f32[2,3,64,2]{3,2,1,0:T(8,128)} %get-tuple-element.234), channel_id=1, source_target_pairs={{9,0},{10,1},{11,2},{12,3},{13,4},{14,5},{15,6},{17,8},{18,9},{19,... | collective-permute-start | bytes 9224 | tf_op jit(solution)/shard_map/while/body/eval_jaxpr/ppermute | solution.py:66
  279.6 7.8 %collective-permute-start = (f32[3,64,2,128]{3,2,1,0:T(2,128)}, f32[3,64,2,128]{3,2,1,0:T(2,128)}, u32[]{:S(2)}, u32[]{:S(2)}) collective-permute-start(f32[3,64,2,128]{3,2,1,0:T(2,128)} %get-tuple-element.225), channel_id=1, source_target_pairs={{8,0},{16,8},{24,16},{32,24},{40,32},{48,40},{56,48},{64,56},{72,6... | collective-permute-start | bytes 589832 | tf_op jit(solution)/shard_map/while/body/eval_jaxpr/ppermute | solution.py:20
  287.5 1.9 collective-permute-start.1
  294.6 2.0 pad.168.fe_ref
  299.9 12.2 %eval_jaxpr.4 = f32[3,64,16,128]{3,2,1,0:T(8,128)S(1)} custom-call(f32[3,68,20,128]{3,2,1,0:T(8,128)S(1)} %select_maximum_fusion.8.xe_ref, f32[3,68,20,128]{3,2,1,0:T(8,128)S(1)} %pad.168.fe_ref, f32[6,64,16,128]{3,2,1,0:T(8,128)S(1)} %copy-done.3, f32[6,64,16,128]{3,2,1,0:T(8,128)S(1)} %copy-done.5, f32[64,16,128]{2,1,0:T(8,128)S(1)} %copy-done.8, ...), custom_call_target="tpu_custom_call" | custom-call | flops 27525120 | bytes 14139392 | tf_op jit(solution)/shard_map/while/body/eval_jaxpr/pallas_call | solution.py:201
  313.7 2.8 collective-permute-start.3
  316.6 8.2 %collective-permute-start.2 = (f32[2,3,64,2]{3,2,1,0:T(8,128)S(1)}, f32[2,3,64,2]{3,2,1,0:T(8,128)S(1)}, u32[]{:S(2)}, u32[]{:S(2)}) collective-permute-start(f32[2,3,64,2]{3,2,1,0:T(8,128)S(1)} %get-tuple-element.231), channel_id=1, source_target_pairs={{8,1},{9,2},{10,3},{11,4},{12,5},{13,6},{14,7},{16,9},{17,10},{18,... | collective-permute-start | bytes 9224 | tf_op jit(solution)/shard_map/while/body/eval_jaxpr/ppermute | solution.py:66
  326.8 2.1 collective-permute-start.6
  329.7 8.9 %collective-permute-start.5 = (f32[2,3,64,2]{3,2,1,0:T(8,128)}, f32[2,3,64,2]{3,2,1,0:T(8,128)S(1)}, u32[]{:S(2)}, u32[]{:S(2)}) collective-permute-start(f32[2,3,64,2]{3,2,1,0:T(8,128)} %get-tuple-element.234), channel_id=1, source_target_pairs={{9,0},{10,1},{11,2},{12,3},{13,4},{14,5},{15,6},{17,8},{18,9},{19,... | collective-permute-start | bytes 9224 | tf_op jit(solution)/shard_map/while/body/eval_jaxpr/ppermute | solution.py:66
  341.6 6.6 %collective-permute-start = (f32[3,64,2,128]{3,2,1,0:T(2,128)}, f32[3,64,2,128]{3,2,1,0:T(2,128)}, u32[]{:S(2)}, u32[]{:S(2)}) collective-permute-start(f32[3,64,2,128]{3,2,1,0:T(2,128)} %get-tuple-element.225), channel_id=1, source_target_pairs={{8,0},{16,8},{24,16},{32,24},{40,32},{48,40},{56,48},{64,56},{72,6... | collective-permute-start | bytes 589832 | tf_op jit(solution)/shard_map/while/body/eval_jaxpr/ppermute | solution.py:20
  348.3 1.9 collective-permute-start.1
  355.3 2.0 pad.168.fe_ref
  360.6 12.2 %eval_jaxpr.4 = f32[3,64,16,128]{3,2,1,0:T(8,128)S(1)} custom-call(f32[3,68,20,128]{3,2,1,0:T(8,128)S(1)} %select_maximum_fusion.8.xe_ref, f32[3,68,20,128]{3,2,1,0:T(8,128)S(1)} %pad.168.fe_ref, f32[6,64,16,128]{3,2,1,0:T(8,128)S(1)} %copy-done.3, f32[6,64,16,128]{3,2,1,0:T(8,128)S(1)} %copy-done.5, f32[64,16,128]{2,1,0:T(8,128)S(1)} %copy-done.8, ...), custom_call_target="tpu_custom_call" | custom-call | flops 27525120 | bytes 14139392 | tf_op jit(solution)/shard_map/while/body/eval_jaxpr/pallas_call | solution.py:201
  (308 shorter events, 110.6 us)
Async XLA Ops:
  4.4 49.1 %collective-permute-start.12 = (f32[2,2,64,16]{3,2,1,0:T(8,128)S(1)}, f32[2,2,64,16]{3,2,1,0:T(8,128)}, u32[]{:S(2)}, u32[]{:S(2)}) collective-permute-start(f32[2,2,64,16]{3,2,1,0:T(8,128)S(1)} %slice.233), channel_id=1, source_target_pairs={{1,0},{2,1},{3,2},{4,3},{5,4},{6,5},{7,6},{9,8},{10,9},{11,10},{12... | collective-permute-start | bytes 49160 | tf_op jit(solution)/shard_map/ppermute | solution.py:20
  10.3 28.4 %collective-permute-start.11 = (f32[2,2,64,2]{3,2,1,0:T(8,128)S(1)}, f32[2,2,64,2]{3,2,1,0:T(8,128)}, u32[]{:S(2)}, u32[]{:S(2)}) collective-permute-start(f32[2,2,64,2]{3,2,1,0:T(8,128)S(1)} %get-tuple-element.159), channel_id=1, source_target_pairs={{1,8},{2,9},{3,10},{4,11},{5,12},{6,13},{7,14},{9,16},{10,17},{11,... | collective-permute-start | bytes 6152 | tf_op jit(solution)/shard_map/ppermute | solution.py:66
  12.2 35.5 %collective-permute-start.13 = (f32[2,2,64,2]{3,2,1,0:T(8,128)}, f32[2,2,64,2]{3,2,1,0:T(8,128)}, u32[]{:S(2)}, u32[]{:S(2)}) collective-permute-start(f32[2,2,64,2]{3,2,1,0:T(8,128)} %get-tuple-element.160), channel_id=1, source_target_pairs={{9,0},{10,1},{11,2},{12,3},{13,4},{14,5},{15,6},{17,8},{18,9},{19,... | collective-permute-start | bytes 6152 | tf_op jit(solution)/shard_map/ppermute | solution.py:66
  19.3 42.2 %collective-permute-start.15 = (f32[2,2,64,16]{3,2,1,0:T(8,128)S(1)}, f32[2,2,64,16]{3,2,1,0:T(8,128)}, u32[]{:S(2)}, u32[]{:S(2)}) collective-permute-start(f32[2,2,64,16]{3,2,1,0:T(8,128)S(1)} %slice.237), channel_id=1, source_target_pairs={{0,1},{1,2},{2,3},{3,4},{4,5},{5,6},{6,7},{8,9},{9,10},{10,11},{11... | collective-permute-start | bytes 49160 | tf_op jit(solution)/shard_map/ppermute | solution.py:20
  36.7 12.9 %collective-permute-start.14 = (f32[2,2,64,2]{3,2,1,0:T(8,128)}, f32[2,2,64,2]{3,2,1,0:T(8,128)S(1)}, u32[]{:S(2)}, u32[]{:S(2)}) collective-permute-start(f32[2,2,64,2]{3,2,1,0:T(8,128)} %get-tuple-element.161), channel_id=1, source_target_pairs={{0,9},{1,10},{2,11},{3,12},{4,13},{5,14},{6,15},{8,17},{9,18},{10,... | collective-permute-start | bytes 6152 | tf_op jit(solution)/shard_map/ppermute | solution.py:66
  38.6 12.9 %collective-permute-start.16 = (f32[2,2,64,2]{3,2,1,0:T(8,128)}, f32[2,2,64,2]{3,2,1,0:T(8,128)S(1)}, u32[]{:S(2)}, u32[]{:S(2)}) collective-permute-start(f32[2,2,64,2]{3,2,1,0:T(8,128)} %get-tuple-element.162), channel_id=1, source_target_pairs={{8,1},{9,2},{10,3},{11,4},{12,5},{13,6},{14,7},{16,9},{17,10},{18,... | collective-permute-start | bytes 6152 | tf_op jit(solution)/shard_map/ppermute | solution.py:66
  47.7 28.2 %collective-permute-start.8 = (f32[65,16,128]{2,1,0:T(8,128)}, f32[65,16,128]{2,1,0:T(8,128)}, u32[]{:S(2)}, u32[]{:S(2)}) collective-permute-start(f32[65,16,128]{2,1,0:T(8,128)} %pad_maximum_fusion.3), channel_id=1, source_target_pairs={{0,1},{1,2},{2,3},{3,4},{4,5},{5,6},{6,7},{8,9},{9,10},{10,11},{11... | collective-permute-start | bytes 1597448 | tf_op jit(solution)/shard_map/ppermute | solution.py:20
  49.7 26.2 %collective-permute-start.9 = (f32[65,16,128]{2,1,0:T(8,128)}, f32[65,16,128]{2,1,0:T(8,128)}, u32[]{:S(2)}, u32[]{:S(2)}) collective-permute-start(f32[65,16,128]{2,1,0:T(8,128)} %pad_maximum_fusion.4), channel_id=1, source_target_pairs={{0,8},{8,16},{16,24},{24,32},{32,40},{40,48},{48,56},{56,64},{64,7... | collective-permute-start | bytes 1597448 | tf_op jit(solution)/shard_map/ppermute | solution.py:20
  51.6 18.3 %collective-permute-start.17 = (f32[2,64,2,128]{3,2,1,0:T(2,128)}, f32[2,64,2,128]{3,2,1,0:T(2,128)}, u32[]{:S(2)}, u32[]{:S(2)}) collective-permute-start(f32[2,64,2,128]{3,2,1,0:T(2,128)} %get-tuple-element.147), channel_id=1, source_target_pairs={{0,8},{8,16},{16,24},{24,32},{32,40},{40,48},{48,56},{56,64},{64,7... | collective-permute-start | bytes 393224 | tf_op jit(solution)/shard_map/ppermute | solution.py:20
  53.5 16.3 %collective-permute-start.18 = (f32[2,64,2,128]{3,2,1,0:T(2,128)S(1)}, f32[2,64,2,128]{3,2,1,0:T(2,128)S(1)}, u32[]{:S(2)}, u32[]{:S(2)}) collective-permute-start(f32[2,64,2,128]{3,2,1,0:T(2,128)S(1)} %get-tuple-element.148), channel_id=1, source_target_pairs={{8,0},{16,8},{24,16},{32,24},{40,32},{48,40},{56,48},{64,56},{72,6... | collective-permute-start | bytes 393224 | tf_op jit(solution)/shard_map/ppermute | solution.py:20
  67.8 16.0 %collective-permute-start.10 = (f32[65,16,128]{2,1,0:T(8,128)S(1)}, f32[65,16,128]{2,1,0:T(8,128)S(1)}, u32[]{:S(2)}, u32[]{:S(2)}) collective-permute-start(f32[65,16,128]{2,1,0:T(8,128)S(1)} %copy-done.12), channel_id=1, source_target_pairs={{0,9},{1,10},{2,11},{3,12},{4,13},{5,14},{6,15},{8,17},{9,18},{10,... | collective-permute-start | bytes 1597448 | tf_op jit(solution)/shard_map/ppermute | solution.py:27
  86.8 36.5 %collective-permute-start.20 = (f32[2,1,64,16]{3,2,0,1:T(8,128)S(1)}, f32[2,1,64,16]{3,2,0,1:T(8,128)S(1)}, u32[]{:S(2)}, u32[]{:S(2)}) collective-permute-start(f32[2,1,64,16]{3,2,0,1:T(8,128)S(1)} %slice.260), channel_id=1, source_target_pairs={{1,0},{2,1},{3,2},{4,3},{5,4},{6,5},{7,6},{9,8},{10,9},{11,10},{12... | collective-permute-start | bytes 24584 | tf_op jit(solution)/shard_map/ppermute | solution.py:20
  91.1 14.6 %collective-permute-start.19 = (f32[2,1,64,2]{3,2,0,1:T(8,128)S(1)}, f32[2,1,64,2]{3,2,0,1:T(8,128)S(1)}, u32[]{:S(2)}, u32[]{:S(2)}) collective-permute-start(f32[2,1,64,2]{3,2,0,1:T(8,128)S(1)} %get-tuple-element.163), channel_id=1, source_target_pairs={{1,8},{2,9},{3,10},{4,11},{5,12},{6,13},{7,14},{9,16},{10,17},{11,... | collective-permute-start | bytes 3080 | tf_op jit(solution)/shard_map/ppermute | solution.py:66
  93.2 30.1 %collective-permute-start.23 = (f32[2,1,64,16]{3,2,0,1:T(8,128)S(1)}, f32[2,1,64,16]{3,2,0,1:T(8,128)S(1)}, u32[]{:S(2)}, u32[]{:S(2)}) collective-permute-start(f32[2,1,64,16]{3,2,0,1:T(8,128)S(1)} %slice.264), channel_id=1, source_target_pairs={{0,1},{1,2},{2,3},{3,4},{4,5},{5,6},{6,7},{8,9},{9,10},{10,11},{11... | collective-permute-start | bytes 24584 | tf_op jit(solution)/shard_map/ppermute | solution.py:20
  95.1 18.4 %collective-permute-start.21 = (f32[2,1,64,2]{3,2,0,1:T(8,128)S(1)}, f32[2,1,64,2]{3,2,0,1:T(8,128)S(1)}, u32[]{:S(2)}, u32[]{:S(2)}) collective-permute-start(f32[2,1,64,2]{3,2,0,1:T(8,128)S(1)} %get-tuple-element.164), channel_id=1, source_target_pairs={{9,0},{10,1},{11,2},{12,3},{13,4},{14,5},{15,6},{17,8},{18,9},{19,... | collective-permute-start | bytes 3080 | tf_op jit(solution)/shard_map/ppermute | solution.py:66
  103.8 11.7 %collective-permute-start.22 = (f32[2,1,64,2]{3,2,0,1:T(8,128)S(1)}, f32[2,1,64,2]{3,2,0,1:T(8,128)S(1)}, u32[]{:S(2)}, u32[]{:S(2)}) collective-permute-start(f32[2,1,64,2]{3,2,0,1:T(8,128)S(1)} %get-tuple-element.165), channel_id=1, source_target_pairs={{0,9},{1,10},{2,11},{3,12},{4,13},{5,14},{6,15},{8,17},{9,18},{10,... | collective-permute-start | bytes 3080 | tf_op jit(solution)/shard_map/ppermute | solution.py:66
  105.8 17.4 %collective-permute-start.24 = (f32[2,1,64,2]{3,2,0,1:T(8,128)S(1)}, f32[2,1,64,2]{3,2,0,1:T(8,128)S(1)}, u32[]{:S(2)}, u32[]{:S(2)}) collective-permute-start(f32[2,1,64,2]{3,2,0,1:T(8,128)S(1)} %get-tuple-element.166), channel_id=1, source_target_pairs={{8,1},{9,2},{10,3},{11,4},{12,5},{13,6},{14,7},{16,9},{17,10},{18,... | collective-permute-start | bytes 3080 | tf_op jit(solution)/shard_map/ppermute | solution.py:66
  113.6 11.3 %collective-permute-start.25 = (f32[1,64,2,128]{3,2,1,0:T(2,128)S(1)}, f32[1,64,2,128]{3,2,1,0:T(2,128)S(1)}, u32[]{:S(2)}, u32[]{:S(2)}) collective-permute-start(f32[1,64,2,128]{3,2,1,0:T(2,128)S(1)} %get-tuple-element.154), channel_id=1, source_target_pairs={{0,8},{8,16},{16,24},{24,32},{32,40},{40,48},{48,56},{56,64},{64,7... | collective-permute-start | bytes 196616 | tf_op jit(solution)/shard_map/ppermute | solution.py:20
  130.7 37.5 %collective-permute-start.3 = (f32[2,3,64,16]{3,2,1,0:T(8,128)S(1)}, f32[2,3,64,16]{3,2,1,0:T(8,128)S(1)}, u32[]{:S(2)}, u32[]{:S(2)}) collective-permute-start(f32[2,3,64,16]{3,2,1,0:T(8,128)S(1)} %slice.524), channel_id=1, source_target_pairs={{0,1},{1,2},{2,3},{3,4},{4,5},{5,6},{6,7},{8,9},{9,10},{10,11},{11... | collective-permute-start | bytes 73736 | tf_op jit(solution)/shard_map/while/body/eval_jaxpr/ppermute | solution.py:20
  132.7 21.5 %collective-permute-start.2 = (f32[2,3,64,2]{3,2,1,0:T(8,128)S(1)}, f32[2,3,64,2]{3,2,1,0:T(8,128)S(1)}, u32[]{:S(2)}, u32[]{:S(2)}) collective-permute-start(f32[2,3,64,2]{3,2,1,0:T(8,128)S(1)} %get-tuple-element.231), channel_id=1, source_target_pairs={{8,1},{9,2},{10,3},{11,4},{12,5},{13,6},{14,7},{16,9},{17,10},{18,... | collective-permute-start | bytes 9224 | tf_op jit(solution)/shard_map/while/body/eval_jaxpr/ppermute | solution.py:66
  138.9 18.3 %collective-permute-start.4 = (f32[2,3,64,2]{3,2,1,0:T(8,128)S(1)}, f32[2,3,64,2]{3,2,1,0:T(8,128)S(1)}, u32[]{:S(2)}, u32[]{:S(2)}) collective-permute-start(f32[2,3,64,2]{3,2,1,0:T(8,128)S(1)} %get-tuple-element.232), channel_id=1, source_target_pairs={{0,9},{1,10},{2,11},{3,12},{4,13},{5,14},{6,15},{8,17},{9,18},{10,... | collective-permute-start | bytes 9224 | tf_op jit(solution)/shard_map/while/body/eval_jaxpr/ppermute | solution.py:66
  140.9 27.4 %collective-permute-start.6 = (f32[2,3,64,16]{3,2,1,0:T(8,128)S(1)}, f32[2,3,64,16]{3,2,1,0:T(8,128)S(1)}, u32[]{:S(2)}, u32[]{:S(2)}) collective-permute-start(f32[2,3,64,16]{3,2,1,0:T(8,128)S(1)} %slice.525), channel_id=1, source_target_pairs={{1,0},{2,1},{3,2},{4,3},{5,4},{6,5},{7,6},{9,8},{10,9},{11,10},{12... | collective-permute-start | bytes 73736 | tf_op jit(solution)/shard_map/while/body/eval_jaxpr/ppermute | solution.py:20
  146.6 19.4 %collective-permute-start.5 = (f32[2,3,64,2]{3,2,1,0:T(8,128)}, f32[2,3,64,2]{3,2,1,0:T(8,128)S(1)}, u32[]{:S(2)}, u32[]{:S(2)}) collective-permute-start(f32[2,3,64,2]{3,2,1,0:T(8,128)} %get-tuple-element.234), channel_id=1, source_target_pairs={{9,0},{10,1},{11,2},{12,3},{13,4},{14,5},{15,6},{17,8},{18,9},{19,... | collective-permute-start | bytes 9224 | tf_op jit(solution)/shard_map/while/body/eval_jaxpr/ppermute | solution.py:66
  154.2 13.9 %collective-permute-start.7 = (f32[2,3,64,2]{3,2,1,0:T(8,128)S(1)}, f32[2,3,64,2]{3,2,1,0:T(8,128)S(1)}, u32[]{:S(2)}, u32[]{:S(2)}) collective-permute-start(f32[2,3,64,2]{3,2,1,0:T(8,128)S(1)} %get-tuple-element.235), channel_id=1, source_target_pairs={{1,8},{2,9},{3,10},{4,11},{5,12},{6,13},{7,14},{9,16},{10,17},{11,... | collective-permute-start | bytes 9224 | tf_op jit(solution)/shard_map/while/body/eval_jaxpr/ppermute | solution.py:66
  157.2 17.9 %collective-permute-start = (f32[3,64,2,128]{3,2,1,0:T(2,128)}, f32[3,64,2,128]{3,2,1,0:T(2,128)}, u32[]{:S(2)}, u32[]{:S(2)}) collective-permute-start(f32[3,64,2,128]{3,2,1,0:T(2,128)} %get-tuple-element.225), channel_id=1, source_target_pairs={{8,0},{16,8},{24,16},{32,24},{40,32},{48,40},{56,48},{64,56},{72,6... | collective-permute-start | bytes 589832 | tf_op jit(solution)/shard_map/while/body/eval_jaxpr/ppermute | solution.py:20
  166.0 10.9 %collective-permute-start.1 = (f32[3,64,2,128]{3,2,1,0:T(2,128)}, f32[3,64,2,128]{3,2,1,0:T(2,128)}, u32[]{:S(2)}, u32[]{:S(2)}) collective-permute-start(f32[3,64,2,128]{3,2,1,0:T(2,128)} %get-tuple-element.226), channel_id=1, source_target_pairs={{0,8},{8,16},{16,24},{24,32},{32,40},{40,48},{48,56},{56,64},{64,7... | collective-permute-start | bytes 589832 | tf_op jit(solution)/shard_map/while/body/eval_jaxpr/ppermute | solution.py:20
  192.2 36.8 %collective-permute-start.3 = (f32[2,3,64,16]{3,2,1,0:T(8,128)S(1)}, f32[2,3,64,16]{3,2,1,0:T(8,128)S(1)}, u32[]{:S(2)}, u32[]{:S(2)}) collective-permute-start(f32[2,3,64,16]{3,2,1,0:T(8,128)S(1)} %slice.524), channel_id=1, source_target_pairs={{0,1},{1,2},{2,3},{3,4},{4,5},{5,6},{6,7},{8,9},{9,10},{10,11},{11... | collective-permute-start | bytes 73736 | tf_op jit(solution)/shard_map/while/body/eval_jaxpr/ppermute | solution.py:20
  194.2 20.8 %collective-permute-start.2 = (f32[2,3,64,2]{3,2,1,0:T(8,128)S(1)}, f32[2,3,64,2]{3,2,1,0:T(8,128)S(1)}, u32[]{:S(2)}, u32[]{:S(2)}) collective-permute-start(f32[2,3,64,2]{3,2,1,0:T(8,128)S(1)} %get-tuple-element.231), channel_id=1, source_target_pairs={{8,1},{9,2},{10,3},{11,4},{12,5},{13,6},{14,7},{16,9},{17,10},{18,... | collective-permute-start | bytes 9224 | tf_op jit(solution)/shard_map/while/body/eval_jaxpr/ppermute | solution.py:66
  200.8 17.1 %collective-permute-start.4 = (f32[2,3,64,2]{3,2,1,0:T(8,128)S(1)}, f32[2,3,64,2]{3,2,1,0:T(8,128)S(1)}, u32[]{:S(2)}, u32[]{:S(2)}) collective-permute-start(f32[2,3,64,2]{3,2,1,0:T(8,128)S(1)} %get-tuple-element.232), channel_id=1, source_target_pairs={{0,9},{1,10},{2,11},{3,12},{4,13},{5,14},{6,15},{8,17},{9,18},{10,... | collective-permute-start | bytes 9224 | tf_op jit(solution)/shard_map/while/body/eval_jaxpr/ppermute | solution.py:66
  202.9 26.2 %collective-permute-start.6 = (f32[2,3,64,16]{3,2,1,0:T(8,128)S(1)}, f32[2,3,64,16]{3,2,1,0:T(8,128)S(1)}, u32[]{:S(2)}, u32[]{:S(2)}) collective-permute-start(f32[2,3,64,16]{3,2,1,0:T(8,128)S(1)} %slice.525), channel_id=1, source_target_pairs={{1,0},{2,1},{3,2},{4,3},{5,4},{6,5},{7,6},{9,8},{10,9},{11,10},{12... | collective-permute-start | bytes 73736 | tf_op jit(solution)/shard_map/while/body/eval_jaxpr/ppermute | solution.py:20
  207.4 19.4 %collective-permute-start.5 = (f32[2,3,64,2]{3,2,1,0:T(8,128)}, f32[2,3,64,2]{3,2,1,0:T(8,128)S(1)}, u32[]{:S(2)}, u32[]{:S(2)}) collective-permute-start(f32[2,3,64,2]{3,2,1,0:T(8,128)} %get-tuple-element.234), channel_id=1, source_target_pairs={{9,0},{10,1},{11,2},{12,3},{13,4},{14,5},{15,6},{17,8},{18,9},{19,... | collective-permute-start | bytes 9224 | tf_op jit(solution)/shard_map/while/body/eval_jaxpr/ppermute | solution.py:66
  215.0 13.9 %collective-permute-start.7 = (f32[2,3,64,2]{3,2,1,0:T(8,128)S(1)}, f32[2,3,64,2]{3,2,1,0:T(8,128)S(1)}, u32[]{:S(2)}, u32[]{:S(2)}) collective-permute-start(f32[2,3,64,2]{3,2,1,0:T(8,128)S(1)} %get-tuple-element.235), channel_id=1, source_target_pairs={{1,8},{2,9},{3,10},{4,11},{5,12},{6,13},{7,14},{9,16},{10,17},{11,... | collective-permute-start | bytes 9224 | tf_op jit(solution)/shard_map/while/body/eval_jaxpr/ppermute | solution.py:66
  217.9 17.9 %collective-permute-start = (f32[3,64,2,128]{3,2,1,0:T(2,128)}, f32[3,64,2,128]{3,2,1,0:T(2,128)}, u32[]{:S(2)}, u32[]{:S(2)}) collective-permute-start(f32[3,64,2,128]{3,2,1,0:T(2,128)} %get-tuple-element.225), channel_id=1, source_target_pairs={{8,0},{16,8},{24,16},{32,24},{40,32},{48,40},{56,48},{64,56},{72,6... | collective-permute-start | bytes 589832 | tf_op jit(solution)/shard_map/while/body/eval_jaxpr/ppermute | solution.py:20
  226.8 10.9 %collective-permute-start.1 = (f32[3,64,2,128]{3,2,1,0:T(2,128)}, f32[3,64,2,128]{3,2,1,0:T(2,128)}, u32[]{:S(2)}, u32[]{:S(2)}) collective-permute-start(f32[3,64,2,128]{3,2,1,0:T(2,128)} %get-tuple-element.226), channel_id=1, source_target_pairs={{0,8},{8,16},{16,24},{24,32},{32,40},{40,48},{48,56},{56,64},{64,7... | collective-permute-start | bytes 589832 | tf_op jit(solution)/shard_map/while/body/eval_jaxpr/ppermute | solution.py:20
  252.9 36.8 %collective-permute-start.3 = (f32[2,3,64,16]{3,2,1,0:T(8,128)S(1)}, f32[2,3,64,16]{3,2,1,0:T(8,128)S(1)}, u32[]{:S(2)}, u32[]{:S(2)}) collective-permute-start(f32[2,3,64,16]{3,2,1,0:T(8,128)S(1)} %slice.524), channel_id=1, source_target_pairs={{0,1},{1,2},{2,3},{3,4},{4,5},{5,6},{6,7},{8,9},{9,10},{10,11},{11... | collective-permute-start | bytes 73736 | tf_op jit(solution)/shard_map/while/body/eval_jaxpr/ppermute | solution.py:20
  255.0 21.6 %collective-permute-start.2 = (f32[2,3,64,2]{3,2,1,0:T(8,128)S(1)}, f32[2,3,64,2]{3,2,1,0:T(8,128)S(1)}, u32[]{:S(2)}, u32[]{:S(2)}) collective-permute-start(f32[2,3,64,2]{3,2,1,0:T(8,128)S(1)} %get-tuple-element.231), channel_id=1, source_target_pairs={{8,1},{9,2},{10,3},{11,4},{12,5},{13,6},{14,7},{16,9},{17,10},{18,... | collective-permute-start | bytes 9224 | tf_op jit(solution)/shard_map/while/body/eval_jaxpr/ppermute | solution.py:66
  262.8 16.8 %collective-permute-start.4 = (f32[2,3,64,2]{3,2,1,0:T(8,128)S(1)}, f32[2,3,64,2]{3,2,1,0:T(8,128)S(1)}, u32[]{:S(2)}, u32[]{:S(2)}) collective-permute-start(f32[2,3,64,2]{3,2,1,0:T(8,128)S(1)} %get-tuple-element.232), channel_id=1, source_target_pairs={{0,9},{1,10},{2,11},{3,12},{4,13},{5,14},{6,15},{8,17},{9,18},{10,... | collective-permute-start | bytes 9224 | tf_op jit(solution)/shard_map/while/body/eval_jaxpr/ppermute | solution.py:66
  264.9 25.0 %collective-permute-start.6 = (f32[2,3,64,16]{3,2,1,0:T(8,128)S(1)}, f32[2,3,64,16]{3,2,1,0:T(8,128)S(1)}, u32[]{:S(2)}, u32[]{:S(2)}) collective-permute-start(f32[2,3,64,16]{3,2,1,0:T(8,128)S(1)} %slice.525), channel_id=1, source_target_pairs={{1,0},{2,1},{3,2},{4,3},{5,4},{6,5},{7,6},{9,8},{10,9},{11,10},{12... | collective-permute-start | bytes 73736 | tf_op jit(solution)/shard_map/while/body/eval_jaxpr/ppermute | solution.py:20
  268.1 19.4 %collective-permute-start.5 = (f32[2,3,64,2]{3,2,1,0:T(8,128)}, f32[2,3,64,2]{3,2,1,0:T(8,128)S(1)}, u32[]{:S(2)}, u32[]{:S(2)}) collective-permute-start(f32[2,3,64,2]{3,2,1,0:T(8,128)} %get-tuple-element.234), channel_id=1, source_target_pairs={{9,0},{10,1},{11,2},{12,3},{13,4},{14,5},{15,6},{17,8},{18,9},{19,... | collective-permute-start | bytes 9224 | tf_op jit(solution)/shard_map/while/body/eval_jaxpr/ppermute | solution.py:66
  276.6 13.0 %collective-permute-start.7 = (f32[2,3,64,2]{3,2,1,0:T(8,128)S(1)}, f32[2,3,64,2]{3,2,1,0:T(8,128)S(1)}, u32[]{:S(2)}, u32[]{:S(2)}) collective-permute-start(f32[2,3,64,2]{3,2,1,0:T(8,128)S(1)} %get-tuple-element.235), channel_id=1, source_target_pairs={{1,8},{2,9},{3,10},{4,11},{5,12},{6,13},{7,14},{9,16},{10,17},{11,... | collective-permute-start | bytes 9224 | tf_op jit(solution)/shard_map/while/body/eval_jaxpr/ppermute | solution.py:66
  279.6 17.0 %collective-permute-start = (f32[3,64,2,128]{3,2,1,0:T(2,128)}, f32[3,64,2,128]{3,2,1,0:T(2,128)}, u32[]{:S(2)}, u32[]{:S(2)}) collective-permute-start(f32[3,64,2,128]{3,2,1,0:T(2,128)} %get-tuple-element.225), channel_id=1, source_target_pairs={{8,0},{16,8},{24,16},{32,24},{40,32},{48,40},{56,48},{64,56},{72,6... | collective-permute-start | bytes 589832 | tf_op jit(solution)/shard_map/while/body/eval_jaxpr/ppermute | solution.py:20
  313.7 36.8 %collective-permute-start.3 = (f32[2,3,64,16]{3,2,1,0:T(8,128)S(1)}, f32[2,3,64,16]{3,2,1,0:T(8,128)S(1)}, u32[]{:S(2)}, u32[]{:S(2)}) collective-permute-start(f32[2,3,64,16]{3,2,1,0:T(8,128)S(1)} %slice.524), channel_id=1, source_target_pairs={{0,1},{1,2},{2,3},{3,4},{4,5},{5,6},{6,7},{8,9},{9,10},{10,11},{11... | collective-permute-start | bytes 73736 | tf_op jit(solution)/shard_map/while/body/eval_jaxpr/ppermute | solution.py:20
  316.6 22.0 %collective-permute-start.2 = (f32[2,3,64,2]{3,2,1,0:T(8,128)S(1)}, f32[2,3,64,2]{3,2,1,0:T(8,128)S(1)}, u32[]{:S(2)}, u32[]{:S(2)}) collective-permute-start(f32[2,3,64,2]{3,2,1,0:T(8,128)S(1)} %get-tuple-element.231), channel_id=1, source_target_pairs={{8,1},{9,2},{10,3},{11,4},{12,5},{13,6},{14,7},{16,9},{17,10},{18,... | collective-permute-start | bytes 9224 | tf_op jit(solution)/shard_map/while/body/eval_jaxpr/ppermute | solution.py:66
  324.8 16.8 %collective-permute-start.4 = (f32[2,3,64,2]{3,2,1,0:T(8,128)S(1)}, f32[2,3,64,2]{3,2,1,0:T(8,128)S(1)}, u32[]{:S(2)}, u32[]{:S(2)}) collective-permute-start(f32[2,3,64,2]{3,2,1,0:T(8,128)S(1)} %get-tuple-element.232), channel_id=1, source_target_pairs={{0,9},{1,10},{2,11},{3,12},{4,13},{5,14},{6,15},{8,17},{9,18},{10,... | collective-permute-start | bytes 9224 | tf_op jit(solution)/shard_map/while/body/eval_jaxpr/ppermute | solution.py:66
  326.8 23.7 %collective-permute-start.6 = (f32[2,3,64,16]{3,2,1,0:T(8,128)S(1)}, f32[2,3,64,16]{3,2,1,0:T(8,128)S(1)}, u32[]{:S(2)}, u32[]{:S(2)}) collective-permute-start(f32[2,3,64,16]{3,2,1,0:T(8,128)S(1)} %slice.525), channel_id=1, source_target_pairs={{1,0},{2,1},{3,2},{4,3},{5,4},{6,5},{7,6},{9,8},{10,9},{11,10},{12... | collective-permute-start | bytes 73736 | tf_op jit(solution)/shard_map/while/body/eval_jaxpr/ppermute | solution.py:20
  329.7 18.6 %collective-permute-start.5 = (f32[2,3,64,2]{3,2,1,0:T(8,128)}, f32[2,3,64,2]{3,2,1,0:T(8,128)S(1)}, u32[]{:S(2)}, u32[]{:S(2)}) collective-permute-start(f32[2,3,64,2]{3,2,1,0:T(8,128)} %get-tuple-element.234), channel_id=1, source_target_pairs={{9,0},{10,1},{11,2},{12,3},{13,4},{14,5},{15,6},{17,8},{18,9},{19,... | collective-permute-start | bytes 9224 | tf_op jit(solution)/shard_map/while/body/eval_jaxpr/ppermute | solution.py:66
  338.6 11.8 %collective-permute-start.7 = (f32[2,3,64,2]{3,2,1,0:T(8,128)S(1)}, f32[2,3,64,2]{3,2,1,0:T(8,128)S(1)}, u32[]{:S(2)}, u32[]{:S(2)}) collective-permute-start(f32[2,3,64,2]{3,2,1,0:T(8,128)S(1)} %get-tuple-element.235), channel_id=1, source_target_pairs={{1,8},{2,9},{3,10},{4,11},{5,12},{6,13},{7,14},{9,16},{10,17},{11,... | collective-permute-start | bytes 9224 | tf_op jit(solution)/shard_map/while/body/eval_jaxpr/ppermute | solution.py:66
  341.6 15.8 %collective-permute-start = (f32[3,64,2,128]{3,2,1,0:T(2,128)}, f32[3,64,2,128]{3,2,1,0:T(2,128)}, u32[]{:S(2)}, u32[]{:S(2)}) collective-permute-start(f32[3,64,2,128]{3,2,1,0:T(2,128)} %get-tuple-element.225), channel_id=1, source_target_pairs={{8,0},{16,8},{24,16},{32,24},{40,32},{48,40},{56,48},{64,56},{72,6... | collective-permute-start | bytes 589832 | tf_op jit(solution)/shard_map/while/body/eval_jaxpr/ppermute | solution.py:20
  (39 other events, 187.1 us)

commit v2 on v0

--- a/solution.py
+++ b/solution.py
@@ -205,9 +205,10 @@
 
     bulk = stiff_lam + stiff_mu
     rate = RELAX_FACTOR / (6.0 * stiff_mu + 3.0 * bulk)
-    moduli = full_pad(*halo(jnp.stack([stiff_mu, bulk])))
-    shear = moduli[0]
-    bulk_pad = moduli[1]
+    padded = full_pad(*halo(jnp.stack([stiff_mu, bulk, joined.astype(jnp.float32)])))
+    shear = padded[0]
+    bulk_pad = padded[1]
+    image = padded[2]
     shear_here = window(shear, 0, 0, 0)
     mean_shear = []
     bulk_beside = []
@@ -221,7 +222,6 @@
     mean_shear = jnp.stack(mean_shear)
     bulk_beside = jnp.stack(bulk_beside)
 
-    image = full_pad(*halo(joined[None].astype(jnp.float32)))[0]
     centre = window(image, 0, 0, 0)
     mismatch = template.astype(jnp.float32) - centre
     slopes = []

time: 275 us -> 279 us (1.015)
  waiting for transfers between devices: 40.6 us -> 60 us
  starting transfers between devices: 107 us -> 93 us
  local copies, waits for them, and re-layouts: 26.6 us -> 22.9 us
    ppermute x26 -> x22, starting transfers between devices: 105 us -> 87.9 us  [shifted_in(): return lax.ppermute(block, axis, route)]
    ppermute x26 -> x22, waiting for transfers between devices: 36.4 us -> 51.3 us  [shifted_in(): return lax.ppermute(block, axis, route)]
    ppermute x1, waiting for transfers between devices: 4.16 us -> 8.7 us  [diagonal_in(): return lax.ppermute(block, ('gx', 'gy'), route)]
    unnamed x5, other arithmetic: 1.7 us -> 5.72 us
    ppermute x1, starting transfers between devices: 2.09 us -> 5.11 us  [diagonal_in(): return lax.ppermute(block, ('gx', 'gy'), route)]
    while x24 -> x16, local copies, waits for them, and re-layouts: 7.18 us -> 4.55 us
    unnamed x33 -> x29, local copies, waits for them, and re-layouts: 8.33 us -> 6.93 us
    dot_general x6 -> x5, matrix products: 7.28 us -> 7.08 us  [halo(): jnp.einsum('kr,ky->ry', arrived, pick, precision=EXACT).reshape(v.shape)]
  transfers between devices with their start and end apart: 27 -> 23, of which waited for: 17 -> 17; matrix products, arithmetic and copies ran while one was open for 11% -> 2% of each run, Pallas kernels for 0% -> 0%
where the time goes in v2:
time: 279 us; the launch traced here: 275 us
  starting transfers between devices  93 us (33%)
  waiting for transfers between devices  60 us (22%)
  Pallas kernels  51.4 us (18%)
  other arithmetic  26.4 us (9%)
  local copies, waits for them, and re-layouts  22.9 us (8%)
  matrix products  19 us (7%)
    ppermute x22, starting transfers between devices, shifted_in(): return lax.ppermute(block, axis, route)  87.9 us
    pallas_call x4, Pallas kernels, relax_call(): pl.pallas_call(relax_kernel, out_shape=out_shape, grid=(depth // chunk,),...  51.4 us
    ppermute x22, waiting for transfers between devices, shifted_in(): return lax.ppermute(block, axis, route)  51.3 us
    ppermute x1, waiting for transfers between devices, diagonal_in(): return lax.ppermute(block, ('gx', 'gy'), route)  8.7 us
    dot_general x5, matrix products, halo(): jnp.einsum('kr,ky->ry', arrived, pick, precision=EXACT).reshape(v.shape)  7.08 us
    unnamed x29, local copies, waits for them, and re-layouts  6.93 us
    unnamed x5, other arithmetic  5.72 us
  transfers between devices with their start and end apart: 23, of which 17 were waited for; matrix products, arithmetic and copies ran while one was open for 2% of the time, Pallas kernels for 0%

profile of v2, /device:TPU:6, one launch (start us, length us, event | category | flops | bytes accessed | tf_op | source)
XLA Modules:
  0.0 275.0 jit_solution(17170480188386197370)
XLA Ops:
  2.5 3.8 %fusion.9 = f32[8,64,16,256]{3,2,0,1:T(8,128)S(1)} fusion(s32[8]{0:T(128)S(1)} %bitcast.132, bf16[8,64,16,128]{3,2,1,0:T(8,128)(2,1)S(1)} %copy-done.5, f32[8,128]{1,0:T(8,128)S(1)} %bitcast_convert_fusion.1, f32[8,16]{1,0:T(8,128)S(1)} %convert_multiply_fusion), kind=kOutput, calls=%fused_computation.19 | convolution fusion | flops 3224895488 | bytes 10490400 | tf_op jit(solution)/shard_map/szxy,syY->szxY/dot_general | solution.py:86
  6.2 3.3 %convolution_bitcast_fusion = f32[64,32,256]{2,1,0:T(8,128)S(1)} fusion(f32[8,64,16,256]{3,2,0,1:T(8,128)S(1)} %fusion.9, s32[8]{0:T(128)S(1)} %bitcast.134), kind=kOutput, calls=%fused_computation.34 | convolution fusion | flops 805314560 | bytes 10485792 | tf_op jit(solution)/shard_map/szxY,sxX->zXY/dot_general | solution.py:87
  9.8 3.6 %collective-permute-start.4 = (f32[65,16,128]{2,1,0:T(8,128)S(1)}, f32[65,16,128]{2,1,0:T(8,128)S(1)}, u32[]{:S(2)}, u32[]{:S(2)}) collective-permute-start(f32[65,16,128]{2,1,0:T(8,128)S(1)} %pad_maximum_fusion.5), channel_id=1, source_target_pairs={{0,1},{1,2},{2,3},{3,4},{4,5},{5,6},{6,7},{8,9},{9,10},{10,11},{11... | collective-permute-start | bytes 1597448 | tf_op jit(solution)/shard_map/ppermute | solution.py:20
  13.5 1.9 collective-permute-start.5
  15.5 5.1 %collective-permute-start.6 = (f32[65,16,128]{2,1,0:T(8,128)S(1)}, f32[65,16,128]{2,1,0:T(8,128)S(1)}, u32[]{:S(2)}, u32[]{:S(2)}) collective-permute-start(f32[65,16,128]{2,1,0:T(8,128)S(1)} %pad_maximum_fusion.7), channel_id=1, source_target_pairs={{0,9},{1,10},{2,11},{3,12},{4,13},{5,14},{6,15},{8,17},{9,18},{10,... | collective-permute-start | bytes 1597448 | tf_op jit(solution)/shard_map/ppermute | solution.py:27
  21.5 7.4 %collective-permute-done.4 = f32[65,16,128]{2,1,0:T(8,128)S(1)} collective-permute-done((f32[65,16,128]{2,1,0:T(8,128)S(1)}, f32[65,16,128]{2,1,0:T(8,128)S(1)}, u32[]{:S(2)}, u32[]{:S(2)}) %collective-permute-start.4) | collective-permute-done | bytes 532512 | tf_op jit(solution)/shard_map/ppermute | solution.py:20
  28.9 8.7 %collective-permute-done.6 = f32[65,16,128]{2,1,0:T(8,128)S(1)} collective-permute-done((f32[65,16,128]{2,1,0:T(8,128)S(1)}, f32[65,16,128]{2,1,0:T(8,128)S(1)}, u32[]{:S(2)}, u32[]{:S(2)}) %collective-permute-start.6) | collective-permute-done | bytes 532512 | tf_op jit(solution)/shard_map/ppermute | solution.py:27
  39.6 6.6 %collective-permute-start.7 = (f32[2,3072]{1,0:T(2,128)S(1)}, f32[2,3072]{1,0:T(2,128)S(1)}, u32[]{:S(2)}, u32[]{:S(2)}) collective-permute-start(f32[2,3072]{1,0:T(2,128)S(1)} %get-tuple-element.157), channel_id=1, source_target_pairs={{1,0},{2,1},{3,2},{4,3},{5,4},{6,5},{7,6},{9,8},{10,9},{11,10},{12... | collective-permute-start | bytes 73736 | tf_op jit(solution)/shard_map/ppermute | solution.py:20
  46.2 1.9 collective-permute-start.8
  48.1 5.9 %collective-permute-done.8 = f32[2,3072]{1,0:T(2,128)S(1)} collective-permute-done((f32[2,3072]{1,0:T(2,128)S(1)}, f32[2,3072]{1,0:T(2,128)S(1)}, u32[]{:S(2)}, u32[]{:S(2)}) %collective-permute-start.8) | collective-permute-done | bytes 24608 | tf_op jit(solution)/shard_map/ppermute | solution.py:20
  56.7 1.9 collective-permute-start.10
  59.6 2.6 collective-permute-start.9
  62.1 2.1 collective-permute-done.10
  64.4 8.2 %collective-permute-done.9 = f32[3,64,4,128]{3,2,1,0:T(4,128)} collective-permute-done((f32[3,64,4,128]{3,2,1,0:T(4,128)}, f32[3,64,4,128]{3,2,1,0:T(4,128)}, u32[]{:S(2)}, u32[]{:S(2)}) %collective-permute-start.9) | collective-permute-done | bytes 393248 | tf_op jit(solution)/shard_map/ppermute | solution.py:20
  75.5 2.0 pad_maximum_fusion.2
  93.7 180.1 %while.13 = (s32[]{:T(128)}, f32[3,64,16,128]{3,2,1,0:T(8,128)S(1)}, f32[6,64,16,128]{3,2,1,0:T(8,128)}, f32[6,64,16,128]{3,2,1,0:T(8,128)}, f32[64,16,128]{2,1,...) while((s32[]{:T(128)}, f32[3,64,16,128]{3,2,1,0:T(8,128)S(1)}, ...), condition=%wide.region_1.2_spmd.clone, body=%wide.region_0.1_spmd.sunk.clone.sunk | while | flops 73839616 | bytes 42041676 | solution.py:238
  94.6 2.0 collective-permute-start
  96.5 6.0 %collective-permute-start.1 = (f32[2,3072]{1,0:T(2,128)S(1)}, f32[2,3072]{1,0:T(2,128)S(1)}, u32[]{:S(2)}, u32[]{:S(2)}) collective-permute-start(f32[2,3072]{1,0:T(2,128)S(1)} %get-tuple-element.213), channel_id=1, source_target_pairs={{1,0},{2,1},{3,2},{4,3},{5,4},{6,5},{7,6},{9,8},{10,9},{11,10},{12... | collective-permute-start | bytes 73736 | tf_op jit(solution)/shard_map/while/body/eval_jaxpr/ppermute | solution.py:20
  102.6 1.5 collective-permute-done.1
  106.8 1.9 collective-permute-start.3
  109.6 7.2 %collective-permute-start.2 = (f32[3,64,4,128]{3,2,1,0:T(4,128)}, f32[3,64,4,128]{3,2,1,0:T(4,128)}, u32[]{:S(2)}, u32[]{:S(2)}) collective-permute-start(f32[3,64,4,128]{3,2,1,0:T(4,128)} %pad_maximum_fusion.12), channel_id=1, source_target_pairs={{8,0},{16,8},{24,16},{32,24},{40,32},{48,40},{56,48},{64,56},{72,6... | collective-permute-start | bytes 1179656 | tf_op jit(solution)/shard_map/while/body/eval_jaxpr/ppermute | solution.py:20
  116.9 2.8 %collective-permute-done.3 = f32[3,64,4,128]{3,2,1,0:T(4,128)S(1)} collective-permute-done((f32[3,64,4,128]{3,2,1,0:T(4,128)}, f32[3,64,4,128]{3,2,1,0:T(4,128)S(1)}, u32[]{:S(2)}, u32[]{:S(2)}) %collective-permute-start.3) | collective-permute-done | bytes 393248 | tf_op jit(solution)/shard_map/while/body/eval_jaxpr/ppermute | solution.py:20
  119.8 2.6 collective-permute-done.2
  125.7 12.9 %eval_jaxpr.4 = f32[3,64,16,128]{3,2,1,0:T(8,128)S(1)} custom-call(f32[3,68,20,128]{3,2,1,0:T(8,128)S(1)} %select_maximum_fusion.12.xe_ref, f32[3,68,20,128]{3,2,1,0:T(8,128)S(1)} %select_maximum_fusion.13.fe_ref, f32[6,64,16,128]{3,2,1,0:T(8,128)} %get-tuple-element.240.mc_ref, f32[6,64,16,128]{3,2,1,0:T(8,128)} %get-tuple-element.241.bc_ref, ...), custom_call_target="tpu_custom_call" | custom-call | flops 27525120 | bytes 14139392 | tf_op jit(solution)/shard_map/while/body/eval_jaxpr/pallas_call | solution.py:164
  139.4 1.9 collective-permute-start
  141.3 6.3 %collective-permute-start.1 = (f32[2,3072]{1,0:T(2,128)S(1)}, f32[2,3072]{1,0:T(2,128)S(1)}, u32[]{:S(2)}, u32[]{:S(2)}) collective-permute-start(f32[2,3072]{1,0:T(2,128)S(1)} %get-tuple-element.213), channel_id=1, source_target_pairs={{1,0},{2,1},{3,2},{4,3},{5,4},{6,5},{7,6},{9,8},{10,9},{11,10},{12... | collective-permute-start | bytes 73736 | tf_op jit(solution)/shard_map/while/body/eval_jaxpr/ppermute | solution.py:20
  147.7 1.5 collective-permute-done.1
  151.9 1.9 collective-permute-start.3
  154.7 7.2 %collective-permute-start.2 = (f32[3,64,4,128]{3,2,1,0:T(4,128)}, f32[3,64,4,128]{3,2,1,0:T(4,128)}, u32[]{:S(2)}, u32[]{:S(2)}) collective-permute-start(f32[3,64,4,128]{3,2,1,0:T(4,128)} %pad_maximum_fusion.12), channel_id=1, source_target_pairs={{8,0},{16,8},{24,16},{32,24},{40,32},{48,40},{56,48},{64,56},{72,6... | collective-permute-start | bytes 1179656 | tf_op jit(solution)/shard_map/while/body/eval_jaxpr/ppermute | solution.py:20
  162.0 2.8 %collective-permute-done.3 = f32[3,64,4,128]{3,2,1,0:T(4,128)S(1)} collective-permute-done((f32[3,64,4,128]{3,2,1,0:T(4,128)}, f32[3,64,4,128]{3,2,1,0:T(4,128)S(1)}, u32[]{:S(2)}, u32[]{:S(2)}) %collective-permute-start.3) | collective-permute-done | bytes 393248 | tf_op jit(solution)/shard_map/while/body/eval_jaxpr/ppermute | solution.py:20
  164.9 2.6 collective-permute-done.2
  170.8 12.9 %eval_jaxpr.4 = f32[3,64,16,128]{3,2,1,0:T(8,128)S(1)} custom-call(f32[3,68,20,128]{3,2,1,0:T(8,128)S(1)} %select_maximum_fusion.12.xe_ref, f32[3,68,20,128]{3,2,1,0:T(8,128)S(1)} %select_maximum_fusion.13.fe_ref, f32[6,64,16,128]{3,2,1,0:T(8,128)} %get-tuple-element.240.mc_ref, f32[6,64,16,128]{3,2,1,0:T(8,128)} %get-tuple-element.241.bc_ref, ...), custom_call_target="tpu_custom_call" | custom-call | flops 27525120 | bytes 14139392 | tf_op jit(solution)/shard_map/while/body/eval_jaxpr/pallas_call | solution.py:164
  184.5 1.9 collective-permute-start
  186.4 6.3 %collective-permute-start.1 = (f32[2,3072]{1,0:T(2,128)S(1)}, f32[2,3072]{1,0:T(2,128)S(1)}, u32[]{:S(2)}, u32[]{:S(2)}) collective-permute-start(f32[2,3072]{1,0:T(2,128)S(1)} %get-tuple-element.213), channel_id=1, source_target_pairs={{1,0},{2,1},{3,2},{4,3},{5,4},{6,5},{7,6},{9,8},{10,9},{11,10},{12... | collective-permute-start | bytes 73736 | tf_op jit(solution)/shard_map/while/body/eval_jaxpr/ppermute | solution.py:20
  192.7 1.5 collective-permute-done.1
  197.0 1.9 collective-permute-start.3
  199.8 7.2 %collective-permute-start.2 = (f32[3,64,4,128]{3,2,1,0:T(4,128)}, f32[3,64,4,128]{3,2,1,0:T(4,128)}, u32[]{:S(2)}, u32[]{:S(2)}) collective-permute-start(f32[3,64,4,128]{3,2,1,0:T(4,128)} %pad_maximum_fusion.12), channel_id=1, source_target_pairs={{8,0},{16,8},{24,16},{32,24},{40,32},{48,40},{56,48},{64,56},{72,6... | collective-permute-start | bytes 1179656 | tf_op jit(solution)/shard_map/while/body/eval_jaxpr/ppermute | solution.py:20
  207.1 2.8 %collective-permute-done.3 = f32[3,64,4,128]{3,2,1,0:T(4,128)S(1)} collective-permute-done((f32[3,64,4,128]{3,2,1,0:T(4,128)}, f32[3,64,4,128]{3,2,1,0:T(4,128)S(1)}, u32[]{:S(2)}, u32[]{:S(2)}) %collective-permute-start.3) | collective-permute-done | bytes 393248 | tf_op jit(solution)/shard_map/while/body/eval_jaxpr/ppermute | solution.py:20
  210.0 2.6 collective-permute-done.2
  215.8 12.9 %eval_jaxpr.4 = f32[3,64,16,128]{3,2,1,0:T(8,128)S(1)} custom-call(f32[3,68,20,128]{3,2,1,0:T(8,128)S(1)} %select_maximum_fusion.12.xe_ref, f32[3,68,20,128]{3,2,1,0:T(8,128)S(1)} %select_maximum_fusion.13.fe_ref, f32[6,64,16,128]{3,2,1,0:T(8,128)} %get-tuple-element.240.mc_ref, f32[6,64,16,128]{3,2,1,0:T(8,128)} %get-tuple-element.241.bc_ref, ...), custom_call_target="tpu_custom_call" | custom-call | flops 27525120 | bytes 14139392 | tf_op jit(solution)/shard_map/while/body/eval_jaxpr/pallas_call | solution.py:164
  229.6 1.9 collective-permute-start
  231.5 6.3 %collective-permute-start.1 = (f32[2,3072]{1,0:T(2,128)S(1)}, f32[2,3072]{1,0:T(2,128)S(1)}, u32[]{:S(2)}, u32[]{:S(2)}) collective-permute-start(f32[2,3072]{1,0:T(2,128)S(1)} %get-tuple-element.213), channel_id=1, source_target_pairs={{1,0},{2,1},{3,2},{4,3},{5,4},{6,5},{7,6},{9,8},{10,9},{11,10},{12... | collective-permute-start | bytes 73736 | tf_op jit(solution)/shard_map/while/body/eval_jaxpr/ppermute | solution.py:20
  237.8 1.5 collective-permute-done.1
  242.1 1.9 collective-permute-start.3
  244.9 7.2 %collective-permute-start.2 = (f32[3,64,4,128]{3,2,1,0:T(4,128)}, f32[3,64,4,128]{3,2,1,0:T(4,128)}, u32[]{:S(2)}, u32[]{:S(2)}) collective-permute-start(f32[3,64,4,128]{3,2,1,0:T(4,128)} %pad_maximum_fusion.12), channel_id=1, source_target_pairs={{8,0},{16,8},{24,16},{32,24},{40,32},{48,40},{56,48},{64,56},{72,6... | collective-permute-start | bytes 1179656 | tf_op jit(solution)/shard_map/while/body/eval_jaxpr/ppermute | solution.py:20
  252.2 2.8 %collective-permute-done.3 = f32[3,64,4,128]{3,2,1,0:T(4,128)S(1)} collective-permute-done((f32[3,64,4,128]{3,2,1,0:T(4,128)}, f32[3,64,4,128]{3,2,1,0:T(4,128)S(1)}, u32[]{:S(2)}, u32[]{:S(2)}) %collective-permute-start.3) | collective-permute-done | bytes 393248 | tf_op jit(solution)/shard_map/while/body/eval_jaxpr/ppermute | solution.py:20
  255.1 2.6 collective-permute-done.2
  260.9 12.9 %eval_jaxpr.4 = f32[3,64,16,128]{3,2,1,0:T(8,128)S(1)} custom-call(f32[3,68,20,128]{3,2,1,0:T(8,128)S(1)} %select_maximum_fusion.12.xe_ref, f32[3,68,20,128]{3,2,1,0:T(8,128)S(1)} %select_maximum_fusion.13.fe_ref, f32[6,64,16,128]{3,2,1,0:T(8,128)} %get-tuple-element.240.mc_ref, f32[6,64,16,128]{3,2,1,0:T(8,128)} %get-tuple-element.241.bc_ref, ...), custom_call_target="tpu_custom_call" | custom-call | flops 27525120 | bytes 14139392 | tf_op jit(solution)/shard_map/while/body/eval_jaxpr/pallas_call | solution.py:164
  (128 shorter events, 59.2 us)
Async XLA Ops:
  0.6 1.8 copy-start.5
  0.6 0.9 copy-start.11
  0.7 0.8 copy-start.10
  0.7 0.9 copy-start.13
  0.7 1.2 copy-start.12
  9.7 10.8 %copy-start.4 = (f32[64,16,128]{2,1,0:T(8,128)S(1)}, f32[64,16,128]{2,1,0:T(8,128)}, u32[]{:S(2)}) copy-start(f32[64,16,128]{2,1,0:T(8,128)} %param.21) | copy-start | bytes 1572868
  9.8 10.8 %copy-start.6 = (f32[64,16,128]{2,1,0:T(8,128)S(1)}, f32[64,16,128]{2,1,0:T(8,128)}, u32[]{:S(2)}) copy-start(f32[64,16,128]{2,1,0:T(8,128)} %param.22) | copy-start | bytes 1572868
  9.8 19.1 %collective-permute-start.4 = (f32[65,16,128]{2,1,0:T(8,128)S(1)}, f32[65,16,128]{2,1,0:T(8,128)S(1)}, u32[]{:S(2)}, u32[]{:S(2)}) collective-permute-start(f32[65,16,128]{2,1,0:T(8,128)S(1)} %pad_maximum_fusion.5), channel_id=1, source_target_pairs={{0,1},{1,2},{2,3},{3,4},{4,5},{5,6},{6,7},{8,9},{9,10},{10,11},{11... | collective-permute-start | bytes 1597448 | tf_op jit(solution)/shard_map/ppermute | solution.py:20
  13.5 15.4 %collective-permute-start.5 = (f32[65,16,128]{2,1,0:T(8,128)S(1)}, f32[65,16,128]{2,1,0:T(8,128)S(1)}, u32[]{:S(2)}, u32[]{:S(2)}) collective-permute-start(f32[65,16,128]{2,1,0:T(8,128)S(1)} %pad_maximum_fusion.6), channel_id=1, source_target_pairs={{0,8},{8,16},{16,24},{24,32},{32,40},{40,48},{48,56},{56,64},{64,7... | collective-permute-start | bytes 1597448 | tf_op jit(solution)/shard_map/ppermute | solution.py:20
  15.5 22.2 %collective-permute-start.6 = (f32[65,16,128]{2,1,0:T(8,128)S(1)}, f32[65,16,128]{2,1,0:T(8,128)S(1)}, u32[]{:S(2)}, u32[]{:S(2)}) collective-permute-start(f32[65,16,128]{2,1,0:T(8,128)S(1)} %pad_maximum_fusion.7), channel_id=1, source_target_pairs={{0,9},{1,10},{2,11},{3,12},{4,13},{5,14},{6,15},{8,17},{9,18},{10,... | collective-permute-start | bytes 1597448 | tf_op jit(solution)/shard_map/ppermute | solution.py:27
  37.8 0.9 copy-start.9
  39.6 8.6 %collective-permute-start.7 = (f32[2,3072]{1,0:T(2,128)S(1)}, f32[2,3072]{1,0:T(2,128)S(1)}, u32[]{:S(2)}, u32[]{:S(2)}) collective-permute-start(f32[2,3072]{1,0:T(2,128)S(1)} %get-tuple-element.157), channel_id=1, source_target_pairs={{1,0},{2,1},{3,2},{4,3},{5,4},{6,5},{7,6},{9,8},{10,9},{11,10},{12... | collective-permute-start | bytes 73736 | tf_op jit(solution)/shard_map/ppermute | solution.py:20
  46.2 7.8 %collective-permute-start.8 = (f32[2,3072]{1,0:T(2,128)S(1)}, f32[2,3072]{1,0:T(2,128)S(1)}, u32[]{:S(2)}, u32[]{:S(2)}) collective-permute-start(f32[2,3072]{1,0:T(2,128)S(1)} %get-tuple-element.158), channel_id=1, source_target_pairs={{0,1},{1,2},{2,3},{3,4},{4,5},{5,6},{6,7},{8,9},{9,10},{10,11},{11... | collective-permute-start | bytes 73736 | tf_op jit(solution)/shard_map/ppermute | solution.py:20
  56.7 7.5 %collective-permute-start.10 = (f32[3,64,4,128]{3,2,1,0:T(4,128)}, f32[3,64,4,128]{3,2,1,0:T(4,128)S(1)}, u32[]{:S(2)}, u32[]{:S(2)}) collective-permute-start(f32[3,64,4,128]{3,2,1,0:T(4,128)} %pad_maximum_fusion.9), channel_id=1, source_target_pairs={{8,0},{16,8},{24,16},{32,24},{40,32},{48,40},{56,48},{64,56},{72,6... | collective-permute-start | bytes 1179656 | tf_op jit(solution)/shard_map/ppermute | solution.py:20
  59.6 13.0 %collective-permute-start.9 = (f32[3,64,4,128]{3,2,1,0:T(4,128)}, f32[3,64,4,128]{3,2,1,0:T(4,128)}, u32[]{:S(2)}, u32[]{:S(2)}) collective-permute-start(f32[3,64,4,128]{3,2,1,0:T(4,128)} %pad_maximum_fusion.8), channel_id=1, source_target_pairs={{0,8},{8,16},{16,24},{24,32},{32,40},{40,48},{48,56},{56,64},{64,7... | collective-permute-start | bytes 1179656 | tf_op jit(solution)/shard_map/ppermute | solution.py:20
  87.3 3.4 %copy-start.7 = (bf16[64,16,128]{2,1,0:T(8,128)(2,1)S(1)}, bf16[64,16,128]{2,1,0:T(8,128)(2,1)}, u32[]{:S(2)}) copy-start(bf16[64,16,128]{2,1,0:T(8,128)(2,1)} %param.20) | copy-start | bytes 786436
  91.8 2.0 copy-start.1
  91.8 2.0 copy-start.8
  94.6 8.0 %collective-permute-start = (f32[2,3072]{1,0:T(2,128)S(1)}, f32[2,3072]{1,0:T(2,128)S(1)}, u32[]{:S(2)}, u32[]{:S(2)}) collective-permute-start(f32[2,3072]{1,0:T(2,128)S(1)} %get-tuple-element.212), channel_id=1, source_target_pairs={{0,1},{1,2},{2,3},{3,4},{4,5},{5,6},{6,7},{8,9},{9,10},{10,11},{11... | collective-permute-start | bytes 73736 | tf_op jit(solution)/shard_map/while/body/eval_jaxpr/ppermute | solution.py:20
  96.5 7.5 %collective-permute-start.1 = (f32[2,3072]{1,0:T(2,128)S(1)}, f32[2,3072]{1,0:T(2,128)S(1)}, u32[]{:S(2)}, u32[]{:S(2)}) collective-permute-start(f32[2,3072]{1,0:T(2,128)S(1)} %get-tuple-element.213), channel_id=1, source_target_pairs={{1,0},{2,1},{3,2},{4,3},{5,4},{6,5},{7,6},{9,8},{10,9},{11,10},{12... | collective-permute-start | bytes 73736 | tf_op jit(solution)/shard_map/while/body/eval_jaxpr/ppermute | solution.py:20
  106.8 12.9 %collective-permute-start.3 = (f32[3,64,4,128]{3,2,1,0:T(4,128)}, f32[3,64,4,128]{3,2,1,0:T(4,128)S(1)}, u32[]{:S(2)}, u32[]{:S(2)}) collective-permute-start(f32[3,64,4,128]{3,2,1,0:T(4,128)} %pad_maximum_fusion.13), channel_id=1, source_target_pairs={{0,8},{8,16},{16,24},{24,32},{32,40},{40,48},{48,56},{56,64},{64,7... | collective-permute-start | bytes 1179656 | tf_op jit(solution)/shard_map/while/body/eval_jaxpr/ppermute | solution.py:20
  109.6 12.8 %collective-permute-start.2 = (f32[3,64,4,128]{3,2,1,0:T(4,128)}, f32[3,64,4,128]{3,2,1,0:T(4,128)}, u32[]{:S(2)}, u32[]{:S(2)}) collective-permute-start(f32[3,64,4,128]{3,2,1,0:T(4,128)} %pad_maximum_fusion.12), channel_id=1, source_target_pairs={{8,0},{16,8},{24,16},{32,24},{40,32},{48,40},{56,48},{64,56},{72,6... | collective-permute-start | bytes 1179656 | tf_op jit(solution)/shard_map/while/body/eval_jaxpr/ppermute | solution.py:20
  124.1 1.4 copy-start.2
  124.2 1.5 copy-start.3
  139.4 8.3 %collective-permute-start = (f32[2,3072]{1,0:T(2,128)S(1)}, f32[2,3072]{1,0:T(2,128)S(1)}, u32[]{:S(2)}, u32[]{:S(2)}) collective-permute-start(f32[2,3072]{1,0:T(2,128)S(1)} %get-tuple-element.212), channel_id=1, source_target_pairs={{0,1},{1,2},{2,3},{3,4},{4,5},{5,6},{6,7},{8,9},{9,10},{10,11},{11... | collective-permute-start | bytes 73736 | tf_op jit(solution)/shard_map/while/body/eval_jaxpr/ppermute | solution.py:20
  141.3 7.8 %collective-permute-start.1 = (f32[2,3072]{1,0:T(2,128)S(1)}, f32[2,3072]{1,0:T(2,128)S(1)}, u32[]{:S(2)}, u32[]{:S(2)}) collective-permute-start(f32[2,3072]{1,0:T(2,128)S(1)} %get-tuple-element.213), channel_id=1, source_target_pairs={{1,0},{2,1},{3,2},{4,3},{5,4},{6,5},{7,6},{9,8},{10,9},{11,10},{12... | collective-permute-start | bytes 73736 | tf_op jit(solution)/shard_map/while/body/eval_jaxpr/ppermute | solution.py:20
  151.9 12.9 %collective-permute-start.3 = (f32[3,64,4,128]{3,2,1,0:T(4,128)}, f32[3,64,4,128]{3,2,1,0:T(4,128)S(1)}, u32[]{:S(2)}, u32[]{:S(2)}) collective-permute-start(f32[3,64,4,128]{3,2,1,0:T(4,128)} %pad_maximum_fusion.13), channel_id=1, source_target_pairs={{0,8},{8,16},{16,24},{24,32},{32,40},{40,48},{48,56},{56,64},{64,7... | collective-permute-start | bytes 1179656 | tf_op jit(solution)/shard_map/while/body/eval_jaxpr/ppermute | solution.py:20
  154.7 12.8 %collective-permute-start.2 = (f32[3,64,4,128]{3,2,1,0:T(4,128)}, f32[3,64,4,128]{3,2,1,0:T(4,128)}, u32[]{:S(2)}, u32[]{:S(2)}) collective-permute-start(f32[3,64,4,128]{3,2,1,0:T(4,128)} %pad_maximum_fusion.12), channel_id=1, source_target_pairs={{8,0},{16,8},{24,16},{32,24},{40,32},{48,40},{56,48},{64,56},{72,6... | collective-permute-start | bytes 1179656 | tf_op jit(solution)/shard_map/while/body/eval_jaxpr/ppermute | solution.py:20
  169.2 1.4 copy-start.2
  169.2 1.5 copy-start.3
  184.5 8.3 %collective-permute-start = (f32[2,3072]{1,0:T(2,128)S(1)}, f32[2,3072]{1,0:T(2,128)S(1)}, u32[]{:S(2)}, u32[]{:S(2)}) collective-permute-start(f32[2,3072]{1,0:T(2,128)S(1)} %get-tuple-element.212), channel_id=1, source_target_pairs={{0,1},{1,2},{2,3},{3,4},{4,5},{5,6},{6,7},{8,9},{9,10},{10,11},{11... | collective-permute-start | bytes 73736 | tf_op jit(solution)/shard_map/while/body/eval_jaxpr/ppermute | solution.py:20
  186.4 7.8 %collective-permute-start.1 = (f32[2,3072]{1,0:T(2,128)S(1)}, f32[2,3072]{1,0:T(2,128)S(1)}, u32[]{:S(2)}, u32[]{:S(2)}) collective-permute-start(f32[2,3072]{1,0:T(2,128)S(1)} %get-tuple-element.213), channel_id=1, source_target_pairs={{1,0},{2,1},{3,2},{4,3},{5,4},{6,5},{7,6},{9,8},{10,9},{11,10},{12... | collective-permute-start | bytes 73736 | tf_op jit(solution)/shard_map/while/body/eval_jaxpr/ppermute | solution.py:20
  197.0 12.9 %collective-permute-start.3 = (f32[3,64,4,128]{3,2,1,0:T(4,128)}, f32[3,64,4,128]{3,2,1,0:T(4,128)S(1)}, u32[]{:S(2)}, u32[]{:S(2)}) collective-permute-start(f32[3,64,4,128]{3,2,1,0:T(4,128)} %pad_maximum_fusion.13), channel_id=1, source_target_pairs={{0,8},{8,16},{16,24},{24,32},{32,40},{40,48},{48,56},{56,64},{64,7... | collective-permute-start | bytes 1179656 | tf_op jit(solution)/shard_map/while/body/eval_jaxpr/ppermute | solution.py:20
  199.8 12.8 %collective-permute-start.2 = (f32[3,64,4,128]{3,2,1,0:T(4,128)}, f32[3,64,4,128]{3,2,1,0:T(4,128)}, u32[]{:S(2)}, u32[]{:S(2)}) collective-permute-start(f32[3,64,4,128]{3,2,1,0:T(4,128)} %pad_maximum_fusion.12), channel_id=1, source_target_pairs={{8,0},{16,8},{24,16},{32,24},{40,32},{48,40},{56,48},{64,56},{72,6... | collective-permute-start | bytes 1179656 | tf_op jit(solution)/shard_map/while/body/eval_jaxpr/ppermute | solution.py:20
  214.3 1.4 copy-start.2
  214.3 1.5 copy-start.3
  229.6 8.3 %collective-permute-start = (f32[2,3072]{1,0:T(2,128)S(1)}, f32[2,3072]{1,0:T(2,128)S(1)}, u32[]{:S(2)}, u32[]{:S(2)}) collective-permute-start(f32[2,3072]{1,0:T(2,128)S(1)} %get-tuple-element.212), channel_id=1, source_target_pairs={{0,1},{1,2},{2,3},{3,4},{4,5},{5,6},{6,7},{8,9},{9,10},{10,11},{11... | collective-permute-start | bytes 73736 | tf_op jit(solution)/shard_map/while/body/eval_jaxpr/ppermute | solution.py:20
  231.5 7.8 %collective-permute-start.1 = (f32[2,3072]{1,0:T(2,128)S(1)}, f32[2,3072]{1,0:T(2,128)S(1)}, u32[]{:S(2)}, u32[]{:S(2)}) collective-permute-start(f32[2,3072]{1,0:T(2,128)S(1)} %get-tuple-element.213), channel_id=1, source_target_pairs={{1,0},{2,1},{3,2},{4,3},{5,4},{6,5},{7,6},{9,8},{10,9},{11,10},{12... | collective-permute-start | bytes 73736 | tf_op jit(solution)/shard_map/while/body/eval_jaxpr/ppermute | solution.py:20
  242.1 12.9 %collective-permute-start.3 = (f32[3,64,4,128]{3,2,1,0:T(4,128)}, f32[3,64,4,128]{3,2,1,0:T(4,128)S(1)}, u32[]{:S(2)}, u32[]{:S(2)}) collective-permute-start(f32[3,64,4,128]{3,2,1,0:T(4,128)} %pad_maximum_fusion.13), channel_id=1, source_target_pairs={{0,8},{8,16},{16,24},{24,32},{32,40},{40,48},{48,56},{56,64},{64,7... | collective-permute-start | bytes 1179656 | tf_op jit(solution)/shard_map/while/body/eval_jaxpr/ppermute | solution.py:20
  244.9 12.8 %collective-permute-start.2 = (f32[3,64,4,128]{3,2,1,0:T(4,128)}, f32[3,64,4,128]{3,2,1,0:T(4,128)}, u32[]{:S(2)}, u32[]{:S(2)}) collective-permute-start(f32[3,64,4,128]{3,2,1,0:T(4,128)} %pad_maximum_fusion.12), channel_id=1, source_target_pairs={{8,0},{16,8},{24,16},{32,24},{40,32},{48,40},{56,48},{64,56},{72,6... | collective-permute-start | bytes 1179656 | tf_op jit(solution)/shard_map/while/body/eval_jaxpr/ppermute | solution.py:20
  259.4 1.4 copy-start.2
  259.4 1.5 copy-start.3
  273.8 1.1 copy-start

commit v3 on v0

--- a/solution.py
+++ b/solution.py
@@ -153,7 +153,7 @@
     lax.fori_loop(0, chunk, body, 0)
 
 
-def relax_call(xe, fe, mc, bc, rate, forcing, chunk=8):
+def relax_call(xe, fe, mc, bc, rate, forcing, chunk=16):
     chans, depth, wide_x, wide_y = forcing.shape
     out_shape = jax.ShapeDtypeStruct(forcing.shape, jnp.float32)
     moved = sum(a.size * a.dtype.itemsize for a in (xe, fe, mc, bc, rate, forcing)) + forcing.size * 4

time: 275 us -> 275 us (level)
  no operation moved by 1% of the time
where the time goes in v3:
time: 275 us; the launch traced here: 271 us
  starting transfers between devices  107 us (39%)
  Pallas kernels  51.4 us (19%)
  waiting for transfers between devices  40.6 us (15%)
  local copies, waits for them, and re-layouts  26.6 us (10%)
  other arithmetic  23.8 us (9%)
  matrix products  19.2 us (7%)
    ppermute x26, starting transfers between devices, shifted_in(): return lax.ppermute(block, axis, route)  105 us
    pallas_call x4, Pallas kernels, relax_call(): pl.pallas_call(relax_kernel, out_shape=out_shape, grid=(depth // chunk,),...  51.4 us
    ppermute x26, waiting for transfers between devices, shifted_in(): return lax.ppermute(block, axis, route)  36.4 us
    unnamed x33, local copies, waits for them, and re-layouts  8.33 us
    dot_general x6, matrix products, halo(): jnp.einsum('kr,ky->ry', arrived, pick, precision=EXACT).reshape(v.shape)  7.28 us
    while x24, local copies, waits for them, and re-layouts  7.18 us
  transfers between devices with their start and end apart: 27, of which 17 were waited for; matrix products, arithmetic and copies ran while one was open for 11% of the time, Pallas kernels for 0%

profile of v3, /device:TPU:6, one launch (start us, length us, event | category | flops | bytes accessed | tf_op | source)
XLA Modules:
  0.0 270.9 jit_solution(9045647349588028659)
XLA Ops:
  3.5 5.2 %collective-permute-start.7 = (f32[2,2048]{1,0:T(2,128)S(1)}, f32[2,2048]{1,0:T(2,128)S(1)}, u32[]{:S(2)}, u32[]{:S(2)}) collective-permute-start(f32[2,2048]{1,0:T(2,128)S(1)} %get-tuple-element.166), channel_id=1, source_target_pairs={{1,0},{2,1},{3,2},{4,3},{5,4},{6,5},{7,6},{9,8},{10,9},{11,10},{12... | collective-permute-start | bytes 49160 | tf_op jit(solution)/shard_map/ppermute | solution.py:20
  8.7 1.9 collective-permute-start.8
  11.4 3.8 %fusion.9 = f32[8,64,16,256]{3,2,0,1:T(8,128)S(1)} fusion(s32[8]{0:T(128)S(1)} %bitcast.138, bf16[8,64,16,128]{3,2,1,0:T(8,128)(2,1)S(1)} %copy-done.7, f32[8,128]{1,0:T(8,128)S(1)} %bitcast_convert_fusion.1, f32[8,16]{1,0:T(8,128)S(1)} %convert_multiply_fusion), kind=kOutput, calls=%fused_computation.18 | convolution fusion | flops 3224895488 | bytes 10490400 | tf_op jit(solution)/shard_map/szxy,syY->szxY/dot_general | solution.py:86
  15.1 3.3 %convolution_bitcast_fusion = f32[64,32,256]{2,1,0:T(8,128)S(1)} fusion(f32[8,64,16,256]{3,2,0,1:T(8,128)S(1)} %fusion.9, s32[8]{0:T(128)S(1)} %bitcast.140), kind=kOutput, calls=%fused_computation.33 | convolution fusion | flops 805314560 | bytes 10485792 | tf_op jit(solution)/shard_map/szxY,sxX->zXY/dot_general | solution.py:87
  19.5 2.2 collective-permute-start.4
  23.8 1.9 collective-permute-start.9
  26.5 3.9 %collective-permute-start.5 = (f32[65,16,128]{2,1,0:T(8,128)}, f32[65,16,128]{2,1,0:T(8,128)}, u32[]{:S(2)}, u32[]{:S(2)}) collective-permute-start(f32[65,16,128]{2,1,0:T(8,128)} %pad_maximum_fusion.6), channel_id=1, source_target_pairs={{0,8},{8,16},{16,24},{24,32},{32,40},{40,48},{48,56},{56,64},{64,7... | collective-permute-start | bytes 1597448 | tf_op jit(solution)/shard_map/ppermute | solution.py:20
  31.3 5.2 %collective-permute-start.10 = (f32[2,64,4,128]{3,2,1,0:T(4,128)}, f32[2,64,4,128]{3,2,1,0:T(4,128)}, u32[]{:S(2)}, u32[]{:S(2)}) collective-permute-start(f32[2,64,4,128]{3,2,1,0:T(4,128)} %pad_maximum_fusion.9), channel_id=1, source_target_pairs={{8,0},{16,8},{24,16},{32,24},{40,32},{48,40},{56,48},{64,56},{72,6... | collective-permute-start | bytes 786440 | tf_op jit(solution)/shard_map/ppermute | solution.py:20
  37.4 2.1 collective-permute-start.6
  51.9 4.2 %collective-permute-done.6 = f32[65,16,128]{2,1,0:T(8,128)S(1)} collective-permute-done((f32[65,16,128]{2,1,0:T(8,128)}, f32[65,16,128]{2,1,0:T(8,128)S(1)}, u32[]{:S(2)}, u32[]{:S(2)}) %collective-permute-start.6) | collective-permute-done | bytes 532512 | tf_op jit(solution)/shard_map/ppermute | solution.py:27
  57.8 3.9 %collective-permute-start.11 = (f32[2,1024]{1,0:T(2,128)S(1)}, f32[2,1024]{1,0:T(2,128)S(1)}, u32[]{:S(2)}, u32[]{:S(2)}) collective-permute-start(f32[2,1024]{1,0:T(2,128)S(1)} %get-tuple-element.172), channel_id=1, source_target_pairs={{1,0},{2,1},{3,2},{4,3},{5,4},{6,5},{7,6},{9,8},{10,9},{11,10},{12... | collective-permute-start | bytes 24584 | tf_op jit(solution)/shard_map/ppermute | solution.py:20
  61.7 2.0 collective-permute-start.12
  64.0 5.3 %collective-permute-done.12 = f32[2,1024]{1,0:T(2,128)S(1)} collective-permute-done((f32[2,1024]{1,0:T(2,128)S(1)}, f32[2,1024]{1,0:T(2,128)S(1)}, u32[]{:S(2)}, u32[]{:S(2)}) %collective-permute-start.12) | collective-permute-done | bytes 8224 | tf_op jit(solution)/shard_map/ppermute | solution.py:20
  70.1 1.9 collective-permute-start.13
  72.5 7.5 %collective-permute-start.14 = (f32[1,64,4,128]{3,2,1,0:T(4,128)S(1)}, f32[1,64,4,128]{3,2,1,0:T(4,128)S(1)}, u32[]{:S(2)}, u32[]{:S(2)}) collective-permute-start(f32[1,64,4,128]{3,2,1,0:T(4,128)S(1)} %pad_maximum_fusion.11), channel_id=1, source_target_pairs={{8,0},{16,8},{24,16},{32,24},{40,32},{48,40},{56,48},{64,56},{72,6... | collective-permute-start | bytes 393224 | tf_op jit(solution)/shard_map/ppermute | solution.py:20
  80.1 2.2 collective-permute-done.14
  86.8 182.9 %while.13 = (s32[]{:T(128)}, f32[3,64,16,128]{3,2,1,0:T(8,128)S(1)}, f32[6,64,16,128]{3,2,1,0:T(8,128)}, f32[6,64,16,128]{3,2,1,0:T(8,128)}, f32[64,16,128]{2,1,...) while((s32[]{:T(128)}, f32[3,64,16,128]{3,2,1,0:T(8,128)S(1)}, ...), condition=%wide.region_1.2_spmd.clone, body=%wide.region_0.1_spmd.sunk.clone.sunk | while | flops 73839616 | bytes 54624616 | solution.py:238
  87.7 1.9 collective-permute-start
  89.6 6.0 %collective-permute-start.1 = (f32[2,3072]{1,0:T(2,128)S(1)}, f32[2,3072]{1,0:T(2,128)S(1)}, u32[]{:S(2)}, u32[]{:S(2)}) collective-permute-start(f32[2,3072]{1,0:T(2,128)S(1)} %get-tuple-element.226), channel_id=1, source_target_pairs={{1,0},{2,1},{3,2},{4,3},{5,4},{6,5},{7,6},{9,8},{10,9},{11,10},{12... | collective-permute-start | bytes 73736 | tf_op jit(solution)/shard_map/while/body/eval_jaxpr/ppermute | solution.py:20
  95.6 1.5 collective-permute-done.1
  99.9 1.9 collective-permute-start.3
  102.7 7.2 %collective-permute-start.2 = (f32[3,64,4,128]{3,2,1,0:T(4,128)}, f32[3,64,4,128]{3,2,1,0:T(4,128)}, u32[]{:S(2)}, u32[]{:S(2)}) collective-permute-start(f32[3,64,4,128]{3,2,1,0:T(4,128)} %pad_maximum_fusion.14), channel_id=1, source_target_pairs={{8,0},{16,8},{24,16},{32,24},{40,32},{48,40},{56,48},{64,56},{72,6... | collective-permute-start | bytes 1179656 | tf_op jit(solution)/shard_map/while/body/eval_jaxpr/ppermute | solution.py:20
  110.0 2.8 %collective-permute-done.3 = f32[3,64,4,128]{3,2,1,0:T(4,128)S(1)} collective-permute-done((f32[3,64,4,128]{3,2,1,0:T(4,128)}, f32[3,64,4,128]{3,2,1,0:T(4,128)S(1)}, u32[]{:S(2)}, u32[]{:S(2)}) %collective-permute-start.3) | collective-permute-done | bytes 393248 | tf_op jit(solution)/shard_map/while/body/eval_jaxpr/ppermute | solution.py:20
  112.9 2.6 collective-permute-done.2
  119.4 12.9 %eval_jaxpr.4 = f32[3,64,16,128]{3,2,1,0:T(8,128)S(1)} custom-call(f32[3,68,20,128]{3,2,1,0:T(8,128)S(1)} %select_maximum_fusion.15.xe_ref, f32[3,68,20,128]{3,2,1,0:T(8,128)S(1)} %select_maximum_fusion.16.fe_ref, f32[6,64,16,128]{3,2,1,0:T(8,128)S(1)} %copy-done.3, f32[6,64,16,128]{3,2,1,0:T(8,128)} %get-tuple-element.254.bc_ref, ...), custom_call_target="tpu_custom_call" | custom-call | flops 27525120 | bytes 14139392 | tf_op jit(solution)/shard_map/while/body/eval_jaxpr/pallas_call | solution.py:164
  133.2 1.9 collective-permute-start
  135.1 6.3 %collective-permute-start.1 = (f32[2,3072]{1,0:T(2,128)S(1)}, f32[2,3072]{1,0:T(2,128)S(1)}, u32[]{:S(2)}, u32[]{:S(2)}) collective-permute-start(f32[2,3072]{1,0:T(2,128)S(1)} %get-tuple-element.226), channel_id=1, source_target_pairs={{1,0},{2,1},{3,2},{4,3},{5,4},{6,5},{7,6},{9,8},{10,9},{11,10},{12... | collective-permute-start | bytes 73736 | tf_op jit(solution)/shard_map/while/body/eval_jaxpr/ppermute | solution.py:20
  141.4 1.5 collective-permute-done.1
  145.7 1.9 collective-permute-start.3
  148.5 7.2 %collective-permute-start.2 = (f32[3,64,4,128]{3,2,1,0:T(4,128)}, f32[3,64,4,128]{3,2,1,0:T(4,128)}, u32[]{:S(2)}, u32[]{:S(2)}) collective-permute-start(f32[3,64,4,128]{3,2,1,0:T(4,128)} %pad_maximum_fusion.14), channel_id=1, source_target_pairs={{8,0},{16,8},{24,16},{32,24},{40,32},{48,40},{56,48},{64,56},{72,6... | collective-permute-start | bytes 1179656 | tf_op jit(solution)/shard_map/while/body/eval_jaxpr/ppermute | solution.py:20
  155.8 2.8 %collective-permute-done.3 = f32[3,64,4,128]{3,2,1,0:T(4,128)S(1)} collective-permute-done((f32[3,64,4,128]{3,2,1,0:T(4,128)}, f32[3,64,4,128]{3,2,1,0:T(4,128)S(1)}, u32[]{:S(2)}, u32[]{:S(2)}) %collective-permute-start.3) | collective-permute-done | bytes 393248 | tf_op jit(solution)/shard_map/while/body/eval_jaxpr/ppermute | solution.py:20
  158.7 2.6 collective-permute-done.2
  165.3 12.9 %eval_jaxpr.4 = f32[3,64,16,128]{3,2,1,0:T(8,128)S(1)} custom-call(f32[3,68,20,128]{3,2,1,0:T(8,128)S(1)} %select_maximum_fusion.15.xe_ref, f32[3,68,20,128]{3,2,1,0:T(8,128)S(1)} %select_maximum_fusion.16.fe_ref, f32[6,64,16,128]{3,2,1,0:T(8,128)S(1)} %copy-done.3, f32[6,64,16,128]{3,2,1,0:T(8,128)} %get-tuple-element.254.bc_ref, ...), custom_call_target="tpu_custom_call" | custom-call | flops 27525120 | bytes 14139392 | tf_op jit(solution)/shard_map/while/body/eval_jaxpr/pallas_call | solution.py:164
  179.0 1.9 collective-permute-start
  180.9 6.3 %collective-permute-start.1 = (f32[2,3072]{1,0:T(2,128)S(1)}, f32[2,3072]{1,0:T(2,128)S(1)}, u32[]{:S(2)}, u32[]{:S(2)}) collective-permute-start(f32[2,3072]{1,0:T(2,128)S(1)} %get-tuple-element.226), channel_id=1, source_target_pairs={{1,0},{2,1},{3,2},{4,3},{5,4},{6,5},{7,6},{9,8},{10,9},{11,10},{12... | collective-permute-start | bytes 73736 | tf_op jit(solution)/shard_map/while/body/eval_jaxpr/ppermute | solution.py:20
  187.2 1.5 collective-permute-done.1
  191.5 1.9 collective-permute-start.3
  194.3 7.2 %collective-permute-start.2 = (f32[3,64,4,128]{3,2,1,0:T(4,128)}, f32[3,64,4,128]{3,2,1,0:T(4,128)}, u32[]{:S(2)}, u32[]{:S(2)}) collective-permute-start(f32[3,64,4,128]{3,2,1,0:T(4,128)} %pad_maximum_fusion.14), channel_id=1, source_target_pairs={{8,0},{16,8},{24,16},{32,24},{40,32},{48,40},{56,48},{64,56},{72,6... | collective-permute-start | bytes 1179656 | tf_op jit(solution)/shard_map/while/body/eval_jaxpr/ppermute | solution.py:20
  201.6 2.8 %collective-permute-done.3 = f32[3,64,4,128]{3,2,1,0:T(4,128)S(1)} collective-permute-done((f32[3,64,4,128]{3,2,1,0:T(4,128)}, f32[3,64,4,128]{3,2,1,0:T(4,128)S(1)}, u32[]{:S(2)}, u32[]{:S(2)}) %collective-permute-start.3) | collective-permute-done | bytes 393248 | tf_op jit(solution)/shard_map/while/body/eval_jaxpr/ppermute | solution.py:20
  204.5 2.6 collective-permute-done.2
  211.1 12.9 %eval_jaxpr.4 = f32[3,64,16,128]{3,2,1,0:T(8,128)S(1)} custom-call(f32[3,68,20,128]{3,2,1,0:T(8,128)S(1)} %select_maximum_fusion.15.xe_ref, f32[3,68,20,128]{3,2,1,0:T(8,128)S(1)} %select_maximum_fusion.16.fe_ref, f32[6,64,16,128]{3,2,1,0:T(8,128)S(1)} %copy-done.3, f32[6,64,16,128]{3,2,1,0:T(8,128)} %get-tuple-element.254.bc_ref, ...), custom_call_target="tpu_custom_call" | custom-call | flops 27525120 | bytes 14139392 | tf_op jit(solution)/shard_map/while/body/eval_jaxpr/pallas_call | solution.py:164
  224.8 1.9 collective-permute-start
  226.7 6.3 %collective-permute-start.1 = (f32[2,3072]{1,0:T(2,128)S(1)}, f32[2,3072]{1,0:T(2,128)S(1)}, u32[]{:S(2)}, u32[]{:S(2)}) collective-permute-start(f32[2,3072]{1,0:T(2,128)S(1)} %get-tuple-element.226), channel_id=1, source_target_pairs={{1,0},{2,1},{3,2},{4,3},{5,4},{6,5},{7,6},{9,8},{10,9},{11,10},{12... | collective-permute-start | bytes 73736 | tf_op jit(solution)/shard_map/while/body/eval_jaxpr/ppermute | solution.py:20
  237.3 1.9 collective-permute-start.3
  240.1 7.2 %collective-permute-start.2 = (f32[3,64,4,128]{3,2,1,0:T(4,128)}, f32[3,64,4,128]{3,2,1,0:T(4,128)}, u32[]{:S(2)}, u32[]{:S(2)}) collective-permute-start(f32[3,64,4,128]{3,2,1,0:T(4,128)} %pad_maximum_fusion.14), channel_id=1, source_target_pairs={{8,0},{16,8},{24,16},{32,24},{40,32},{48,40},{56,48},{64,56},{72,6... | collective-permute-start | bytes 1179656 | tf_op jit(solution)/shard_map/while/body/eval_jaxpr/ppermute | solution.py:20
  247.4 2.8 %collective-permute-done.3 = f32[3,64,4,128]{3,2,1,0:T(4,128)S(1)} collective-permute-done((f32[3,64,4,128]{3,2,1,0:T(4,128)}, f32[3,64,4,128]{3,2,1,0:T(4,128)S(1)}, u32[]{:S(2)}, u32[]{:S(2)}) %collective-permute-start.3) | collective-permute-done | bytes 393248 | tf_op jit(solution)/shard_map/while/body/eval_jaxpr/ppermute | solution.py:20
  250.3 2.6 collective-permute-done.2
  256.9 12.9 %eval_jaxpr.4 = f32[3,64,16,128]{3,2,1,0:T(8,128)S(1)} custom-call(f32[3,68,20,128]{3,2,1,0:T(8,128)S(1)} %select_maximum_fusion.15.xe_ref, f32[3,68,20,128]{3,2,1,0:T(8,128)S(1)} %select_maximum_fusion.16.fe_ref, f32[6,64,16,128]{3,2,1,0:T(8,128)S(1)} %copy-done.3, f32[6,64,16,128]{3,2,1,0:T(8,128)} %get-tuple-element.254.bc_ref, ...), custom_call_target="tpu_custom_call" | custom-call | flops 27525120 | bytes 14139392 | tf_op jit(solution)/shard_map/while/body/eval_jaxpr/pallas_call | solution.py:164
  (160 shorter events, 65.2 us)
Async XLA Ops:
  2.8 8.5 %copy-start.13 = (bf16[8,1,128]{2,0,1:T(8,128)(2,1)S(1)}, bf16[8,1,128]{2,0,1:T(8,128)(2,1)}, u32[]{:S(2)}) copy-start(bf16[8,1,128]{2,0,1:T(8,128)(2,1)} %param.17) | copy-start | bytes 6148
  2.8 8.5 %copy-start.14 = (bf16[8,1,16]{2,0,1:T(8,128)(2,1)S(1)}, bf16[8,1,16]{2,0,1:T(8,128)(2,1)}, u32[]{:S(2)}) copy-start(bf16[8,1,16]{2,0,1:T(8,128)(2,1)} %param.16) | copy-start | bytes 772
  2.8 8.6 %copy-start.7 = (bf16[8,64,16,128]{3,2,1,0:T(8,128)(2,1)S(1)}, bf16[8,64,16,128]{3,2,1,0:T(8,128)(2,1)}, u32[]{:S(2)}) copy-start(bf16[8,64,16,128]{3,2,1,0:T(8,128)(2,1)} %param.15) | copy-start | bytes 6291460
  2.8 8.6 %copy-start.15 = (s32[8,1,1]{0,2,1:T(1,128)S(1)}, s32[8,1,1]{0,2,1:T(1,128)}, u32[]{:S(2)}) copy-start(s32[8,1,1]{0,2,1:T(1,128)} %param.19) | copy-start | bytes 100
  3.5 18.3 %collective-permute-start.7 = (f32[2,2048]{1,0:T(2,128)S(1)}, f32[2,2048]{1,0:T(2,128)S(1)}, u32[]{:S(2)}, u32[]{:S(2)}) collective-permute-start(f32[2,2048]{1,0:T(2,128)S(1)} %get-tuple-element.166), channel_id=1, source_target_pairs={{1,0},{2,1},{3,2},{4,3},{5,4},{6,5},{7,6},{9,8},{10,9},{11,10},{12... | collective-permute-start | bytes 49160 | tf_op jit(solution)/shard_map/ppermute | solution.py:20
  8.7 13.1 %collective-permute-start.8 = (f32[2,2048]{1,0:T(2,128)S(1)}, f32[2,2048]{1,0:T(2,128)S(1)}, u32[]{:S(2)}, u32[]{:S(2)}) collective-permute-start(f32[2,2048]{1,0:T(2,128)S(1)} %get-tuple-element.167), channel_id=1, source_target_pairs={{0,1},{1,2},{2,3},{3,4},{4,5},{5,6},{6,7},{8,9},{9,10},{10,11},{11... | collective-permute-start | bytes 49160 | tf_op jit(solution)/shard_map/ppermute | solution.py:20
  11.3 3.8 %copy-start.16 = (s32[8,1,1]{0,2,1:T(1,128)S(1)}, s32[8,1,1]{0,2,1:T(1,128)}, u32[]{:S(2)}) copy-start(s32[8,1,1]{0,2,1:T(1,128)} %param.18) | copy-start | bytes 100
  19.5 32.4 %collective-permute-start.4 = (f32[65,16,128]{2,1,0:T(8,128)S(1)}, f32[65,16,128]{2,1,0:T(8,128)}, u32[]{:S(2)}, u32[]{:S(2)}) collective-permute-start(f32[65,16,128]{2,1,0:T(8,128)S(1)} %pad_maximum_fusion.5), channel_id=1, source_target_pairs={{0,1},{1,2},{2,3},{3,4},{4,5},{5,6},{6,7},{8,9},{9,10},{10,11},{11... | collective-permute-start | bytes 1597448 | tf_op jit(solution)/shard_map/ppermute | solution.py:20
  23.8 15.7 %collective-permute-start.9 = (f32[2,64,4,128]{3,2,1,0:T(4,128)}, f32[2,64,4,128]{3,2,1,0:T(4,128)S(1)}, u32[]{:S(2)}, u32[]{:S(2)}) collective-permute-start(f32[2,64,4,128]{3,2,1,0:T(4,128)} %pad_maximum_fusion.8), channel_id=1, source_target_pairs={{0,8},{8,16},{16,24},{24,32},{32,40},{40,48},{48,56},{56,64},{64,7... | collective-permute-start | bytes 786440 | tf_op jit(solution)/shard_map/ppermute | solution.py:20
  26.5 25.4 %collective-permute-start.5 = (f32[65,16,128]{2,1,0:T(8,128)}, f32[65,16,128]{2,1,0:T(8,128)}, u32[]{:S(2)}, u32[]{:S(2)}) collective-permute-start(f32[65,16,128]{2,1,0:T(8,128)} %pad_maximum_fusion.6), channel_id=1, source_target_pairs={{0,8},{8,16},{16,24},{24,32},{32,40},{40,48},{48,56},{56,64},{64,7... | collective-permute-start | bytes 1597448 | tf_op jit(solution)/shard_map/ppermute | solution.py:20
  31.3 9.4 %collective-permute-start.10 = (f32[2,64,4,128]{3,2,1,0:T(4,128)}, f32[2,64,4,128]{3,2,1,0:T(4,128)}, u32[]{:S(2)}, u32[]{:S(2)}) collective-permute-start(f32[2,64,4,128]{3,2,1,0:T(4,128)} %pad_maximum_fusion.9), channel_id=1, source_target_pairs={{8,0},{16,8},{24,16},{32,24},{40,32},{48,40},{56,48},{64,56},{72,6... | collective-permute-start | bytes 786440 | tf_op jit(solution)/shard_map/ppermute | solution.py:20
  37.4 18.7 %collective-permute-start.6 = (f32[65,16,128]{2,1,0:T(8,128)}, f32[65,16,128]{2,1,0:T(8,128)S(1)}, u32[]{:S(2)}, u32[]{:S(2)}) collective-permute-start(f32[65,16,128]{2,1,0:T(8,128)} %pad_maximum_fusion.7), channel_id=1, source_target_pairs={{0,9},{1,10},{2,11},{3,12},{4,13},{5,14},{6,15},{8,17},{9,18},{10,... | collective-permute-start | bytes 1597448 | tf_op jit(solution)/shard_map/ppermute | solution.py:27
  57.6 4.1 %copy-start.9 = (bf16[64,16,128]{2,1,0:T(8,128)(2,1)}, bf16[64,16,128]{2,1,0:T(8,128)(2,1)S(1)}, u32[]{:S(2)}) copy-start(bf16[64,16,128]{2,1,0:T(8,128)(2,1)S(1)} %get-tuple-element.122) | copy-start | bytes 786436
  57.8 6.2 %collective-permute-start.11 = (f32[2,1024]{1,0:T(2,128)S(1)}, f32[2,1024]{1,0:T(2,128)S(1)}, u32[]{:S(2)}, u32[]{:S(2)}) collective-permute-start(f32[2,1024]{1,0:T(2,128)S(1)} %get-tuple-element.172), channel_id=1, source_target_pairs={{1,0},{2,1},{3,2},{4,3},{5,4},{6,5},{7,6},{9,8},{10,9},{11,10},{12... | collective-permute-start | bytes 24584 | tf_op jit(solution)/shard_map/ppermute | solution.py:20
  61.7 7.7 %collective-permute-start.12 = (f32[2,1024]{1,0:T(2,128)S(1)}, f32[2,1024]{1,0:T(2,128)S(1)}, u32[]{:S(2)}, u32[]{:S(2)}) collective-permute-start(f32[2,1024]{1,0:T(2,128)S(1)} %get-tuple-element.173), channel_id=1, source_target_pairs={{0,1},{1,2},{2,3},{3,4},{4,5},{5,6},{6,7},{8,9},{9,10},{10,11},{11... | collective-permute-start | bytes 24584 | tf_op jit(solution)/shard_map/ppermute | solution.py:20
  70.1 9.9 %collective-permute-start.13 = (f32[1,64,4,128]{3,2,1,0:T(4,128)S(1)}, f32[1,64,4,128]{3,2,1,0:T(4,128)S(1)}, u32[]{:S(2)}, u32[]{:S(2)}) collective-permute-start(f32[1,64,4,128]{3,2,1,0:T(4,128)S(1)} %pad_maximum_fusion.10), channel_id=1, source_target_pairs={{0,8},{8,16},{16,24},{24,32},{32,40},{40,48},{48,56},{56,64},{64,7... | collective-permute-start | bytes 393224 | tf_op jit(solution)/shard_map/ppermute | solution.py:20
  72.4 10.3 %copy-start.2 = (f32[6,64,16,128]{3,2,1,0:T(8,128)}, f32[6,64,16,128]{3,2,1,0:T(8,128)S(1)}, u32[]{:S(2)}) copy-start(f32[6,64,16,128]{3,2,1,0:T(8,128)S(1)} %fusion.35) | copy-start | bytes 9437188
  72.5 9.8 %collective-permute-start.14 = (f32[1,64,4,128]{3,2,1,0:T(4,128)S(1)}, f32[1,64,4,128]{3,2,1,0:T(4,128)S(1)}, u32[]{:S(2)}, u32[]{:S(2)}) collective-permute-start(f32[1,64,4,128]{3,2,1,0:T(4,128)S(1)} %pad_maximum_fusion.11), channel_id=1, source_target_pairs={{8,0},{16,8},{24,16},{32,24},{40,32},{48,40},{56,48},{64,56},{72,6... | collective-permute-start | bytes 393224 | tf_op jit(solution)/shard_map/ppermute | solution.py:20
  84.8 2.0 copy-start.1
  84.8 2.0 copy-start.11
  87.7 8.0 %collective-permute-start = (f32[2,3072]{1,0:T(2,128)S(1)}, f32[2,3072]{1,0:T(2,128)S(1)}, u32[]{:S(2)}, u32[]{:S(2)}) collective-permute-start(f32[2,3072]{1,0:T(2,128)S(1)} %get-tuple-element.225), channel_id=1, source_target_pairs={{0,1},{1,2},{2,3},{3,4},{4,5},{5,6},{6,7},{8,9},{9,10},{10,11},{11... | collective-permute-start | bytes 73736 | tf_op jit(solution)/shard_map/while/body/eval_jaxpr/ppermute | solution.py:20
  89.6 7.5 %collective-permute-start.1 = (f32[2,3072]{1,0:T(2,128)S(1)}, f32[2,3072]{1,0:T(2,128)S(1)}, u32[]{:S(2)}, u32[]{:S(2)}) collective-permute-start(f32[2,3072]{1,0:T(2,128)S(1)} %get-tuple-element.226), channel_id=1, source_target_pairs={{1,0},{2,1},{3,2},{4,3},{5,4},{6,5},{7,6},{9,8},{10,9},{11,10},{12... | collective-permute-start | bytes 73736 | tf_op jit(solution)/shard_map/while/body/eval_jaxpr/ppermute | solution.py:20
  99.9 12.9 %collective-permute-start.3 = (f32[3,64,4,128]{3,2,1,0:T(4,128)}, f32[3,64,4,128]{3,2,1,0:T(4,128)S(1)}, u32[]{:S(2)}, u32[]{:S(2)}) collective-permute-start(f32[3,64,4,128]{3,2,1,0:T(4,128)} %pad_maximum_fusion.15), channel_id=1, source_target_pairs={{0,8},{8,16},{16,24},{24,32},{32,40},{40,48},{48,56},{56,64},{64,7... | collective-permute-start | bytes 1179656 | tf_op jit(solution)/shard_map/while/body/eval_jaxpr/ppermute | solution.py:20
  102.7 12.8 %collective-permute-start.2 = (f32[3,64,4,128]{3,2,1,0:T(4,128)}, f32[3,64,4,128]{3,2,1,0:T(4,128)}, u32[]{:S(2)}, u32[]{:S(2)}) collective-permute-start(f32[3,64,4,128]{3,2,1,0:T(4,128)} %pad_maximum_fusion.14), channel_id=1, source_target_pairs={{8,0},{16,8},{24,16},{32,24},{40,32},{48,40},{56,48},{64,56},{72,6... | collective-permute-start | bytes 1179656 | tf_op jit(solution)/shard_map/while/body/eval_jaxpr/ppermute | solution.py:20
  116.9 1.4 copy-start.4
  117.3 2.1 copy-start.3
  117.3 2.2 copy-start.5
  133.2 8.3 %collective-permute-start = (f32[2,3072]{1,0:T(2,128)S(1)}, f32[2,3072]{1,0:T(2,128)S(1)}, u32[]{:S(2)}, u32[]{:S(2)}) collective-permute-start(f32[2,3072]{1,0:T(2,128)S(1)} %get-tuple-element.225), channel_id=1, source_target_pairs={{0,1},{1,2},{2,3},{3,4},{4,5},{5,6},{6,7},{8,9},{9,10},{10,11},{11... | collective-permute-start | bytes 73736 | tf_op jit(solution)/shard_map/while/body/eval_jaxpr/ppermute | solution.py:20
  135.1 7.8 %collective-permute-start.1 = (f32[2,3072]{1,0:T(2,128)S(1)}, f32[2,3072]{1,0:T(2,128)S(1)}, u32[]{:S(2)}, u32[]{:S(2)}) collective-permute-start(f32[2,3072]{1,0:T(2,128)S(1)} %get-tuple-element.226), channel_id=1, source_target_pairs={{1,0},{2,1},{3,2},{4,3},{5,4},{6,5},{7,6},{9,8},{10,9},{11,10},{12... | collective-permute-start | bytes 73736 | tf_op jit(solution)/shard_map/while/body/eval_jaxpr/ppermute | solution.py:20
  145.7 12.9 %collective-permute-start.3 = (f32[3,64,4,128]{3,2,1,0:T(4,128)}, f32[3,64,4,128]{3,2,1,0:T(4,128)S(1)}, u32[]{:S(2)}, u32[]{:S(2)}) collective-permute-start(f32[3,64,4,128]{3,2,1,0:T(4,128)} %pad_maximum_fusion.15), channel_id=1, source_target_pairs={{0,8},{8,16},{16,24},{24,32},{32,40},{40,48},{48,56},{56,64},{64,7... | collective-permute-start | bytes 1179656 | tf_op jit(solution)/shard_map/while/body/eval_jaxpr/ppermute | solution.py:20
  148.5 12.8 %collective-permute-start.2 = (f32[3,64,4,128]{3,2,1,0:T(4,128)}, f32[3,64,4,128]{3,2,1,0:T(4,128)}, u32[]{:S(2)}, u32[]{:S(2)}) collective-permute-start(f32[3,64,4,128]{3,2,1,0:T(4,128)} %pad_maximum_fusion.14), channel_id=1, source_target_pairs={{8,0},{16,8},{24,16},{32,24},{40,32},{48,40},{56,48},{64,56},{72,6... | collective-permute-start | bytes 1179656 | tf_op jit(solution)/shard_map/while/body/eval_jaxpr/ppermute | solution.py:20
  162.7 1.4 copy-start.4
  163.1 2.1 copy-start.3
  163.1 2.2 copy-start.5
  179.0 8.3 %collective-permute-start = (f32[2,3072]{1,0:T(2,128)S(1)}, f32[2,3072]{1,0:T(2,128)S(1)}, u32[]{:S(2)}, u32[]{:S(2)}) collective-permute-start(f32[2,3072]{1,0:T(2,128)S(1)} %get-tuple-element.225), channel_id=1, source_target_pairs={{0,1},{1,2},{2,3},{3,4},{4,5},{5,6},{6,7},{8,9},{9,10},{10,11},{11... | collective-permute-start | bytes 73736 | tf_op jit(solution)/shard_map/while/body/eval_jaxpr/ppermute | solution.py:20
  180.9 7.8 %collective-permute-start.1 = (f32[2,3072]{1,0:T(2,128)S(1)}, f32[2,3072]{1,0:T(2,128)S(1)}, u32[]{:S(2)}, u32[]{:S(2)}) collective-permute-start(f32[2,3072]{1,0:T(2,128)S(1)} %get-tuple-element.226), channel_id=1, source_target_pairs={{1,0},{2,1},{3,2},{4,3},{5,4},{6,5},{7,6},{9,8},{10,9},{11,10},{12... | collective-permute-start | bytes 73736 | tf_op jit(solution)/shard_map/while/body/eval_jaxpr/ppermute | solution.py:20
  191.5 12.9 %collective-permute-start.3 = (f32[3,64,4,128]{3,2,1,0:T(4,128)}, f32[3,64,4,128]{3,2,1,0:T(4,128)S(1)}, u32[]{:S(2)}, u32[]{:S(2)}) collective-permute-start(f32[3,64,4,128]{3,2,1,0:T(4,128)} %pad_maximum_fusion.15), channel_id=1, source_target_pairs={{0,8},{8,16},{16,24},{24,32},{32,40},{40,48},{48,56},{56,64},{64,7... | collective-permute-start | bytes 1179656 | tf_op jit(solution)/shard_map/while/body/eval_jaxpr/ppermute | solution.py:20
  194.3 12.8 %collective-permute-start.2 = (f32[3,64,4,128]{3,2,1,0:T(4,128)}, f32[3,64,4,128]{3,2,1,0:T(4,128)}, u32[]{:S(2)}, u32[]{:S(2)}) collective-permute-start(f32[3,64,4,128]{3,2,1,0:T(4,128)} %pad_maximum_fusion.14), channel_id=1, source_target_pairs={{8,0},{16,8},{24,16},{32,24},{40,32},{48,40},{56,48},{64,56},{72,6... | collective-permute-start | bytes 1179656 | tf_op jit(solution)/shard_map/while/body/eval_jaxpr/ppermute | solution.py:20
  208.5 1.4 copy-start.4
  208.9 2.1 copy-start.3
  208.9 2.2 copy-start.5
  224.8 8.3 %collective-permute-start = (f32[2,3072]{1,0:T(2,128)S(1)}, f32[2,3072]{1,0:T(2,128)S(1)}, u32[]{:S(2)}, u32[]{:S(2)}) collective-permute-start(f32[2,3072]{1,0:T(2,128)S(1)} %get-tuple-element.225), channel_id=1, source_target_pairs={{0,1},{1,2},{2,3},{3,4},{4,5},{5,6},{6,7},{8,9},{9,10},{10,11},{11... | collective-permute-start | bytes 73736 | tf_op jit(solution)/shard_map/while/body/eval_jaxpr/ppermute | solution.py:20
  226.7 7.8 %collective-permute-start.1 = (f32[2,3072]{1,0:T(2,128)S(1)}, f32[2,3072]{1,0:T(2,128)S(1)}, u32[]{:S(2)}, u32[]{:S(2)}) collective-permute-start(f32[2,3072]{1,0:T(2,128)S(1)} %get-tuple-element.226), channel_id=1, source_target_pairs={{1,0},{2,1},{3,2},{4,3},{5,4},{6,5},{7,6},{9,8},{10,9},{11,10},{12... | collective-permute-start | bytes 73736 | tf_op jit(solution)/shard_map/while/body/eval_jaxpr/ppermute | solution.py:20
  237.3 12.9 %collective-permute-start.3 = (f32[3,64,4,128]{3,2,1,0:T(4,128)}, f32[3,64,4,128]{3,2,1,0:T(4,128)S(1)}, u32[]{:S(2)}, u32[]{:S(2)}) collective-permute-start(f32[3,64,4,128]{3,2,1,0:T(4,128)} %pad_maximum_fusion.15), channel_id=1, source_target_pairs={{0,8},{8,16},{16,24},{24,32},{32,40},{40,48},{48,56},{56,64},{64,7... | collective-permute-start | bytes 1179656 | tf_op jit(solution)/shard_map/while/body/eval_jaxpr/ppermute | solution.py:20
  240.1 12.8 %collective-permute-start.2 = (f32[3,64,4,128]{3,2,1,0:T(4,128)}, f32[3,64,4,128]{3,2,1,0:T(4,128)}, u32[]{:S(2)}, u32[]{:S(2)}) collective-permute-start(f32[3,64,4,128]{3,2,1,0:T(4,128)} %pad_maximum_fusion.14), channel_id=1, source_target_pairs={{8,0},{16,8},{24,16},{32,24},{40,32},{48,40},{56,48},{64,56},{72,6... | collective-permute-start | bytes 1179656 | tf_op jit(solution)/shard_map/while/body/eval_jaxpr/ppermute | solution.py:20
  254.3 1.4 copy-start.4
  254.7 2.1 copy-start.3
  254.7 2.2 copy-start.5
  (5 other events, 5.3 us)
